TPU v7x, 256 devices: a whole 4x4x8 slice. The times are simulated.
256 devices in a mesh: group: 2 (over core), dp: 16 (over y, x), tensor: 8 (over z).
Axes of the slice: x: 4, y: 4, z: 8, core: 2. Of those that a mesh axis runs over, the one named last changes fastest.
Arguments:
- stream: bfloat16 [512, 8192], P('tensor', ('group', 'dp'))
- norm_attn: bfloat16 [8192], P(('group', 'dp')), may hold values from 0.29882812 to 3
- norm_ffn: bfloat16 [8192], P(('group', 'dp')), may hold values from 0.29882812 to 3
- w_query: bfloat16 [8192, 8192], P(('group', 'dp'), 'tensor'), may hold values from -0.0625 to 0.0625
- w_keyval: bfloat16 [8192, 2048], P(('group', 'dp'), 'tensor'), may hold values from -0.0625 to 0.0625
- w_out: bfloat16 [8192, 8192], P('tensor', ('group', 'dp')), may hold values from -0.0625 to 0.0625
- w_gate: bfloat16 [8192, 28672], P(('group', 'dp'), 'tensor'), may hold values from -0.0625 to 0.0625
- w_up: bfloat16 [8192, 28672], P(('group', 'dp'), 'tensor'), may hold values from -0.0625 to 0.0625
- w_down: bfloat16 [28672, 8192], P('tensor', ('group', 'dp')), may hold values from -0.03125 to 0.03125
- cache: bfloat16 [512, 8, 256, 256], P(('group', 'dp'), 'tensor')
- lengths: int32 [512], P(('group', 'dp')), may hold values from 1 to 256, as said below
- location: int32 [512], P(('group', 'dp')), may hold values from 0 to 511, as said below
Outputs:
- updated: float32 [512, 8192], P('tensor', ('group', 'dp'))
Inputs may be any that keep to these rules, and one draw needn't show every extreme that they name: Each of the 512 slots is named by exactly one request. Slot s belongs to owner s // 16. Requests r of one aligned block of 16 (one device's requests) that share an owner have different values of location modulo 2; in every draw 2 of them share an owner. `lengths`: some slot holds 256 valid positions in every draw.
All inputs are finite; a program needn't handle non-finite values.
Results may differ from a plain program's by a relative error of at most 0.005.
The roundings to bfloat16 on the way count: a program that leaves them out, or rounds other values in their place, can miss the bound.
Values may be sent and summed in bfloat16 or wider, within the bound.
No kernel may reach another device: no remote copies, remote signals or barrier semaphores. Data moves between devices by JAX's collectives and lax.ppermute only.
A program may use at most 64 MiB of HBM per device.

v0:
```python
import jax
import jax.numpy as jnp
from jax import lax
from jax.sharding import PartitionSpec as P

D = 8192
CAP = 2


EPSILON = 1e-05


def normed(values, gain):
    squares = lax.psum(jnp.sum(values * values, axis=1), ("group", "dp"))
    scale = lax.rsqrt(squares / D + EPSILON)
    return (values * scale[:, None] * gain.astype(jnp.float32)[None, :]).astype(jnp.bfloat16)


def width_sum(normal_rows, matrices):
    gathered = lax.all_gather(normal_rows, "tensor", axis=0, tiled=True)
    return lax.psum_scatter(
        jnp.concatenate(
            [jnp.dot(gathered, matrix, preferred_element_type=jnp.float32) for matrix in matrices],
            axis=1,
        ),
        ("group", "dp"),
        scatter_dimension=0,
        tiled=True,
    )


def project_rows(local_rows, matrix):
    partial_sum = jnp.dot(
        lax.all_gather(local_rows, ("group", "dp"), axis=0, tiled=True),
        matrix,
        preferred_element_type=jnp.float32,
    )
    return lax.psum_scatter(partial_sum, "tensor", scatter_dimension=0, tiled=True)


def attend(query, fresh, stored, counts):
    items = query.shape[0]
    kv_local = stored.shape[1]
    head_size = stored.shape[3] // 2
    grouped = query.reshape(items, kv_local, -1, head_size)
    fresh = fresh.reshape(items, kv_local, 2 * head_size)
    scale = head_size ** (-0.5)
    scores = (
        jnp.einsum(
            "mkgd,mkpd->mkgp", grouped, stored[..., :head_size], preferred_element_type=jnp.float32
        )
        * scale
    )
    own = (
        jnp.einsum(
            "mkgd,mkd->mkg", grouped, fresh[..., :head_size], preferred_element_type=jnp.float32
        )
        * scale
    )
    place = jnp.arange(stored.shape[2], dtype=jnp.int32)
    valid = place[None, None, None, :] < counts[:, None, None, None]
    top = jnp.maximum(jnp.max(jnp.where(valid, scores, -1e30), axis=3), own)
    expo = jnp.where(valid, jnp.exp(scores - top[..., None]), 0.0)
    own_expo = jnp.exp(own - top)
    total = jnp.sum(expo, axis=3) + own_expo
    probs = (expo / total[..., None]).astype(jnp.bfloat16)
    own_prob = (own_expo / total).astype(jnp.bfloat16)
    mixed = jnp.einsum(
        "mkgp,mkpd->mkgd", probs, stored[..., head_size:], preferred_element_type=jnp.float32
    )
    mixed = mixed + own_prob.astype(jnp.float32)[..., None] * fresh[:, :, None, head_size:].astype(
        jnp.float32
    )
    return mixed.reshape(items, -1).astype(jnp.bfloat16)


def per_device(
    stream,
    norm_attn,
    norm_ffn,
    w_query,
    w_keyval,
    w_out,
    w_gate,
    w_up,
    w_down,
    cache,
    lengths,
    location,
):
    owners = lax.axis_size(("group", "dp"))
    per_owner = cache.shape[0]
    resid = stream.astype(jnp.float32)
    attn_in = normed(resid, norm_attn)
    joined = width_sum(attn_in, (w_query, w_keyval))
    query_cols = w_query.shape[1]
    query = joined[:, :query_cols].astype(jnp.bfloat16)
    fresh = joined[:, query_cols:].astype(jnp.bfloat16)
    fresh_cols = fresh.shape[1]
    target = location // per_owner
    place = target * CAP + location % per_owner % CAP
    slot = location % per_owner
    send_query = (
        jnp.zeros((owners * CAP, query_cols), jnp.bfloat16)
        .at[place]
        .set(query)
        .reshape(owners, CAP, query_cols)
    )
    send_fresh = (
        jnp.zeros((owners * CAP, fresh_cols), jnp.bfloat16)
        .at[place]
        .set(fresh)
        .reshape(owners, CAP, fresh_cols)
    )
    send_slot = jnp.zeros((owners * CAP,), jnp.int32).at[place].set(slot).reshape(owners, CAP)
    got_query = lax.all_to_all(send_query, ("group", "dp"), split_axis=0, concat_axis=0, tiled=True)
    got_fresh = lax.all_to_all(send_fresh, ("group", "dp"), split_axis=0, concat_axis=0, tiled=True)
    got_slot = lax.all_to_all(send_slot, ("group", "dp"), split_axis=0, concat_axis=0, tiled=True)
    sources = got_slot.shape[0]
    count = got_slot.shape[1]
    flat_slot = got_slot.reshape(-1)
    answer = attend(
        got_query.reshape(sources * count, -1),
        got_fresh.reshape(sources * count, -1),
        cache[flat_slot],
        lengths[flat_slot],
    )
    answer = answer.reshape(sources, count, -1)
    returned = lax.all_to_all(answer, ("group", "dp"), split_axis=0, concat_axis=0, tiled=True)
    attended = returned.reshape(owners * CAP, -1)[place]
    middle = resid + project_rows(attended, w_out)
    ffn_in = normed(middle, norm_ffn)
    both = width_sum(ffn_in, (w_gate, w_up))
    hidden_cols = w_gate.shape[1]
    hidden = (jax.nn.silu(both[:, :hidden_cols]) * both[:, hidden_cols:]).astype(jnp.bfloat16)
    return middle + project_rows(hidden, w_down)


def solution(mesh):
    placed = (
        P("tensor", ("group", "dp")),
        P(("group", "dp")),
        P(("group", "dp")),
        P(("group", "dp"), "tensor"),
        P(("group", "dp"), "tensor"),
        P("tensor", ("group", "dp")),
        P(("group", "dp"), "tensor"),
        P(("group", "dp"), "tensor"),
        P("tensor", ("group", "dp")),
        P(("group", "dp"), "tensor", None, None),
        P(("group", "dp")),
        P(("group", "dp")),
    )
    return jax.shard_map(
        per_device,
        mesh=mesh,
        in_specs=placed,
        out_specs=P("tensor", ("group", "dp")),
        check_vma=False,
    )
```

profile of v0, /device:TPU:1, one launch (start us, length us, event | category | flops | bytes accessed | tf_op | source)
XLA Modules:
  0.0 639.8 jit_solution(16838073562884392161)
XLA Ops:
  6.5 1.0 fusion.11
  7.6 69.0 %psum.14 = f32[64]{0:T(128)S(1)} all-reduce(f32[64]{0:T(128)S(1)} %fusion.11), channel_id=1, replica_groups=mesh['group'=2,'dp'=16,'tensor'=8] {'group','dp'}, use_global_device_ids=true, to_apply=%region_2.0 | all-reduce | flops 64 | bytes 512 | tf_op jit(solution)/shard_map/psum | solution.py:14
  76.6 0.7 convert_element_type.51
  77.2 0.8 fusion.13
  78.1 22.2 %all_gather.12 = bf16[512,256]{1,0:T(8,128)(2,1)S(1)} all-gather(bf16[64,256]{1,0:T(8,128)(2,1)S(1)} %fusion.13), channel_id=1, replica_groups=mesh['group'=2,'dp'=16,'tensor'=8] {'tensor'}, dimensions={0}, use_global_device_ids=true | all-gather | bytes 294912 | tf_op jit(solution)/shard_map/all_gather | solution.py:20
  100.3 1.1 fusion.33
  101.4 1.5 fusion.32
  102.9 1.7 pad_maximum_fusion.1
  104.6 0.0 reduce-scatter.5.cloned.1.call-update
  104.7 0.6 scatter_custom_fusion
  105.3 0.1 all_to_all.15
  105.4 15.9 %all_to_all.24 = s32[32,1,2]{2,1,0:T(1,128)S(1)} all-to-all(s32[32,1,2]{2,1,0:T(1,128)S(1)} %bitcast.51), channel_id=1, replica_groups=mesh['group'=2,'dp'=16,'tensor'=8] {'group','dp'}, dimensions={0} | all-to-all | bytes 512 | tf_op jit(solution)/shard_map/all_to_all | solution.py:118
  121.3 0.5 broadcast.136
  121.8 0.7 reduce.7
  122.5 0.1 reshape.143
  122.6 0.8 gather_fusion
  123.4 66.9 %reduce-scatter.5.cloned.1.call-done = f32[16,1280]{1,0:T(8,128)} async-done(((f32[512,1280]{1,0:T(8,128)}), f32[16,1280]{1,0:T(8,128)}) %reduce-scatter.5.cloned.1.call-update) | async-done | bytes 81936 | tf_op jit(solution)/shard_map/reduce_scatter | solution.py:21
  190.3 0.9 convert.5
  191.2 0.7 scatter_custom_fusion.2
  191.9 0.6 reshape.147
  192.5 7.4 %all-to-all-start.2 = ((bf16[32,2,256]{2,1,0:T(2,128)(2,1)}), bf16[32,2,256]{2,1,0:T(2,128)(2,1)S(1)}, u32[]{:S(2)}, u32[]{:S(2)}) async-start(bf16[32,2,256]{2,1,0:T(2,128)(2,1)} %reshape.147), calls=%async_computation.3 | async-start | bytes 65536 | tf_op jit(solution)/shard_map/all_to_all | solution.py:117
  199.9 0.1 iota_compare_fusion
  200.0 5.3 gather_fusion.1
  205.4 0.7 scatter_custom_fusion.1
  206.1 0.7 reshape.144
  206.8 0.1 all-to-all-done.2
  206.9 7.2 %all-to-all-start.1 = ((bf16[32,2,1024]{2,1,0:T(2,128)(2,1)}), bf16[32,2,1024]{2,1,0:T(2,128)(2,1)S(1)}, u32[]{:S(2)}, u32[]{:S(2)}) async-start(bf16[32,2,1024]{2,1,0:T(2,128)(2,1)} %reshape.144), calls=%async_computation.2 | async-start | bytes 262144 | tf_op jit(solution)/shard_map/all_to_all | solution.py:116
  214.2 7.5 %all-to-all-done.1 = bf16[32,2,1024]{2,1,0:T(2,128)(2,1)S(1)} async-done(((bf16[32,2,1024]{2,1,0:T(2,128)(2,1)}), bf16[32,2,1024]{2,1,0:T(2,128)(2,1)S(1)}, u32[]{:S(2)}, u32[]{:S(2)}) %all-to-all-start.1) | async-done | bytes 131104 | tf_op jit(solution)/shard_map/all_to_all | solution.py:116
  221.7 0.1 reshape.145
  221.8 0.2 fusion.17
  222.0 3.5 select_reduce_fusion
  225.5 0.3 fusion.5
  225.8 3.0 fusion.4
  228.8 0.7 convert_element_type.59
  229.5 4.1 all-to-all-start.3
  233.6 0.0 all-gather.6.cloned.1.call-start
  233.7 7.5 %all-to-all-done.3 = bf16[32,2,1024]{2,1,0:T(2,128)(2,1)S(1)} async-done(((bf16[32,2,1024]{2,1,0:T(2,128)(2,1)}), bf16[32,2,1024]{2,1,0:T(2,128)(2,1)S(1)}, u32[]{:S(2)}, u32[]{:S(2)}) %all-to-all-start.3) | async-done | bytes 131104 | tf_op jit(solution)/shard_map/all_to_all | solution.py:129
  241.1 0.1 reshape.150
  241.2 1.2 gather_fusion.2
  242.4 0.0 all-gather.6.cloned.1.call-update
  242.4 0.0 reduce-scatter.7.cloned.1.call-start
  242.5 45.6 %all-gather.6.cloned.1.call-done = bf16[512,1024]{1,0:T(8,128)(2,1)} async-done(((bf16[16,1024]{1,0:T(8,128)(2,1)}), bf16[512,1024]{1,0:T(8,128)(2,1)}) %all-gather.6.cloned.1.call-update) | async-done | bytes 1048592 | tf_op jit(solution)/shard_map/all_gather | solution.py:34
  288.1 2.5 fusion.34
  290.6 0.0 reduce-scatter.7.cloned.1.call-update
  290.6 0.0 reduce-scatter.9.cloned.1.call-start
  290.7 32.1 %reduce-scatter.7.cloned.1.call-done = f32[64,256]{1,0:T(8,128)} async-done(((f32[512,256]{1,0:T(8,128)}), f32[64,256]{1,0:T(8,128)}) %reduce-scatter.7.cloned.1.call-update) | async-done | bytes 65552 | tf_op jit(solution)/shard_map/reduce_scatter | solution.py:38
  322.8 0.9 multiply_reduce_fusion
  323.8 72.5 %psum.15 = f32[64]{0:T(128)S(1)} all-reduce(f32[64]{0:T(128)S(1)} %multiply_reduce_fusion), channel_id=1, replica_groups=mesh['group'=2,'dp'=16,'tensor'=8] {'group','dp'}, use_global_device_ids=true, to_apply=%region_10.11 | all-reduce | flops 64 | bytes 512 | tf_op jit(solution)/shard_map/psum | solution.py:14
  396.3 0.9 multiply_convert_fusion
  397.2 18.8 %all_gather.14 = bf16[512,256]{1,0:T(8,128)(2,1)S(1)} all-gather(bf16[64,256]{1,0:T(8,128)(2,1)S(1)} %multiply_convert_fusion), channel_id=1, replica_groups=mesh['group'=2,'dp'=16,'tensor'=8] {'tensor'}, dimensions={0}, use_global_device_ids=true | all-gather | bytes 294912 | tf_op jit(solution)/shard_map/all_gather | solution.py:20
  416.1 2.8 fusion.36
  418.8 1.1 fusion.35
  420.0 5.5 pad_maximum_fusion
  425.5 0.0 reduce-scatter.9.cloned.1.call-update
  425.5 0.0 all-gather.4.cloned.1.call-start
  425.5 115.3 %reduce-scatter.9.cloned.1.call-done = f32[16,7168]{1,0:T(8,128)} async-done(((f32[512,7168]{1,0:T(8,128)}), f32[16,7168]{1,0:T(8,128)}) %reduce-scatter.9.cloned.1.call-update) | async-done | bytes 458768 | tf_op jit(solution)/shard_map/reduce_scatter | solution.py:21
  540.8 1.8 fusion.10
  542.5 0.0 all-gather.4.cloned.1.call-update
  542.6 0.0 reduce-scatter.11.cloned.1.call-start
  542.6 52.1 %all-gather.4.cloned.1.call-done = bf16[512,3584]{1,0:T(8,128)(2,1)} async-done(((bf16[16,3584]{1,0:T(8,128)(2,1)}), bf16[512,3584]{1,0:T(8,128)(2,1)}) %all-gather.4.cloned.1.call-update) | async-done | bytes 3670032 | tf_op jit(solution)/shard_map/all_gather | solution.py:34
  594.7 4.5 fusion.37
  599.2 0.0 reduce-scatter.11.cloned.1.call-update
  599.3 32.2 %reduce-scatter.11.cloned.1.call-done = f32[64,256]{1,0:T(8,128)} async-done(((f32[512,256]{1,0:T(8,128)}), f32[64,256]{1,0:T(8,128)}) %reduce-scatter.11.cloned.1.call-update) | async-done | bytes 65552 | tf_op jit(solution)/shard_map/reduce_scatter | solution.py:38
  631.5 1.5 fusion.19
  (28 shorter events, 0.2 us)
Async XLA Ops:
  6.5 193.5 %copy-start = (bf16[16,1,256,256]{3,2,1,0:T(8,128)(2,1)S(1)}, bf16[16,1,256,256]{3,2,1,0:T(8,128)(2,1)}, u32[]{:S(2)}) copy-start(bf16[16,1,256,256]{3,2,1,0:T(8,128)(2,1)} %param.21) | copy-start | bytes 6291460
  6.5 183.8 %reduce-scatter.5.cloned.1.call-start = ((), (), s32[]{:S(2)}) async-start(), calls=%async_computation.8 | async-start | bytes 2703360 | tf_op jit(solution)/shard_map/reduce_scatter | solution.py:21
  102.9 1.8 copy-start.6
  102.9 19.7 %copy-start.1 = (s32[16]{0:T(128)S(1)}, s32[16]{0:T(128)}, u32[]{:S(2)}) copy-start(s32[16]{0:T(128)} %param.22) | copy-start | bytes 196
  192.5 14.4 %all-to-all-start.2 = ((bf16[32,2,256]{2,1,0:T(2,128)(2,1)}), bf16[32,2,256]{2,1,0:T(2,128)(2,1)S(1)}, u32[]{:S(2)}, u32[]{:S(2)}) async-start(bf16[32,2,256]{2,1,0:T(2,128)(2,1)} %reshape.147), calls=%async_computation.3 | async-start | bytes 65536 | tf_op jit(solution)/shard_map/all_to_all | solution.py:117
  206.9 14.8 %all-to-all-start.1 = ((bf16[32,2,1024]{2,1,0:T(2,128)(2,1)}), bf16[32,2,1024]{2,1,0:T(2,128)(2,1)S(1)}, u32[]{:S(2)}, u32[]{:S(2)}) async-start(bf16[32,2,1024]{2,1,0:T(2,128)(2,1)} %reshape.144), calls=%async_computation.2 | async-start | bytes 262144 | tf_op jit(solution)/shard_map/all_to_all | solution.py:116
  225.8 62.4 %copy-start.5 = (bf16[1024,256]{1,0:T(8,128)(2,1)S(1)}, bf16[1024,256]{1,0:T(8,128)(2,1)}, u32[]{:S(2)}) copy-start(bf16[1024,256]{1,0:T(8,128)(2,1)} %param.17) | copy-start | bytes 1572868
  225.8 64.9 %copy-start.7 = (bf16[256]{0:T(256)(128)(2,1)S(1)}, bf16[256]{0:T(256)(128)(2,1)}, u32[]{:S(2)}) copy-start(bf16[256]{0:T(256)(128)(2,1)} %param.14) | copy-start | bytes 1540
  225.8 97.0 %copy-start.3 = (bf16[64,256]{1,0:T(8,128)(2,1)S(1)}, bf16[64,256]{1,0:T(8,128)(2,1)}, u32[]{:S(2)}) copy-start(bf16[64,256]{1,0:T(8,128)(2,1)} %param.12) | copy-start | bytes 98308
  229.5 11.7 %all-to-all-start.3 = ((bf16[32,2,1024]{2,1,0:T(2,128)(2,1)}), bf16[32,2,1024]{2,1,0:T(2,128)(2,1)S(1)}, u32[]{:S(2)}, u32[]{:S(2)}) async-start(bf16[32,2,1024]{2,1,0:T(2,128)(2,1)} %convert_element_type.59), calls=%async_computation.4 | async-start | bytes 262144 | tf_op jit(solution)/shard_map/all_to_all | solution.py:129
  233.6 54.5 %all-gather.6.cloned.1.call-start = ((), (), s32[]{:S(2)}) async-start(), calls=%async_computation.13 | async-start | bytes 1081344 | tf_op jit(solution)/shard_map/all_gather | solution.py:34
  242.4 80.4 %reduce-scatter.7.cloned.1.call-start = ((), (), s32[]{:S(2)}) async-start(), calls=%async_computation.9 | async-start | bytes 589824 | tf_op jit(solution)/shard_map/reduce_scatter | solution.py:38
  290.6 250.2 %reduce-scatter.9.cloned.1.call-start = ((), (), s32[]{:S(2)}) async-start(), calls=%async_computation.10 | async-start | bytes 15138816 | tf_op jit(solution)/shard_map/reduce_scatter | solution.py:21
  416.1 2.8 copy-start.2
  425.5 169.2 %all-gather.4.cloned.1.call-start = ((), (), s32[]{:S(2)}) async-start(), calls=%async_computation.11 | async-start | bytes 3784704 | tf_op jit(solution)/shard_map/all_gather | solution.py:34
  542.6 88.9 %copy-start.4 = (f32[64,256]{1,0:T(8,128)S(1)}, f32[64,256]{1,0:T(8,128)}, u32[]{:S(2)}) copy-start(f32[64,256]{1,0:T(8,128)} %reduce-scatter.7.cloned.1.call-done) | copy-start | bytes 196612
  542.6 88.9 %reduce-scatter.11.cloned.1.call-start = ((), (), s32[]{:S(2)}) async-start(), calls=%async_computation.12 | async-start | bytes 589824 | tf_op jit(solution)/shard_map/reduce_scatter | solution.py:38
Sparse Core Ops, SparseCore 0:
  104.8 85.5 reduce-scatter.4
  242.6 45.5 all-gather.5
  290.8 32.0 reduce-scatter.6
  425.6 115.1 reduce-scatter.8
  543.2 51.4 all-gather.3
  599.4 32.0 reduce-scatter.10
where the time goes:
time: 645 us; the launch traced here: 640 us
  waiting for transfers between devices  359 us (56%)
  blocking collectives  198 us (31%)
  matrix products  20.1 us (3%)
  starting transfers between devices  19 us (3%)
  other arithmetic  16.8 us (3%)
  between operations  13.8 us (2%)
  local copies, waits for them, and re-layouts  12.3 us (2%)
    reduce_scatter x2, waiting for transfers between devices, width_sum(): lax.psum_scatter(jnp.concatenate([jnp.dot(gathered, matrix, preferred_ele...  182 us
    psum x2, blocking collectives, normed(): squares = lax.psum(jnp.sum(values * values, axis=1), ('group', 'dp'))  142 us
    all_gather x2, waiting for transfers between devices, project_rows(): lax.all_gather(local_rows, ('group', 'dp'), axis=0, tiled=True)  97.7 us
    reduce_scatter x2, waiting for transfers between devices, project_rows(): lax.psum_scatter(partial_sum, 'tensor', scatter_dimension=0, tiled=True)  64.3 us
    all_gather x2, blocking collectives, width_sum(): gathered = lax.all_gather(normal_rows, 'tensor', axis=0, tiled=True)  41 us
    all_to_all x1, blocking collectives, per_device(): lax.all_to_all(send_slot, ('group', 'dp'), split_axis=0, concat_axis=0, t...  15.9 us
  transfers between devices with their start and end apart: 9, of which 9 were waited for; matrix products, arithmetic and copies ran while one was open for 2% of the time, Pallas kernels for 0%

commit v1 on v0

v1 whole, which is shorter than its diff:
```python
import jax
import jax.numpy as jnp
from jax import lax
from jax.sharding import PartitionSpec as P

D = 8192
WIDTH = ("group", "dp")

EPSILON = 1e-05


def gather_width(values):
    owners = lax.axis_size(WIDTH)
    sent = jnp.broadcast_to(values[None], (owners,) + values.shape)
    return lax.all_to_all(sent, WIDTH, 0, 0, tiled=True)


def scale_rows(values, squares, gain):
    scale = lax.rsqrt(squares / D + EPSILON)
    return (values * scale[:, None] * gain.astype(jnp.float32)[None, :]).astype(jnp.bfloat16)


def reduce_rows(partial, axis):
    parts = lax.axis_size(axis)
    blocks = partial.reshape((parts, partial.shape[0] // parts) + partial.shape[1:])
    return jnp.sum(lax.all_to_all(blocks, axis, 0, 0, tiled=True), axis=0)


def attend(query, fresh, stored, counts):
    items = query.shape[0]
    kv_local = stored.shape[1]
    head_size = stored.shape[3] // 2
    grouped = query.reshape(items, kv_local, -1, head_size)
    fresh = fresh.reshape(items, kv_local, 2 * head_size)
    scale = head_size ** (-0.5)
    scores = (
        jnp.einsum(
            "mkgd,mkpd->mkgp", grouped, stored[..., :head_size], preferred_element_type=jnp.float32
        )
        * scale
    )
    own = (
        jnp.einsum(
            "mkgd,mkd->mkg", grouped, fresh[..., :head_size], preferred_element_type=jnp.float32
        )
        * scale
    )
    place = jnp.arange(stored.shape[2], dtype=jnp.int32)
    valid = place[None, None, None, :] < counts[:, None, None, None]
    top = jnp.maximum(jnp.max(jnp.where(valid, scores, -1e30), axis=3), own)
    expo = jnp.where(valid, jnp.exp(scores - top[..., None]), 0.0)
    own_expo = jnp.exp(own - top)
    total = jnp.sum(expo, axis=3) + own_expo
    probs = (expo / total[..., None]).astype(jnp.bfloat16)
    own_prob = (own_expo / total).astype(jnp.bfloat16)
    mixed = jnp.einsum(
        "mkgp,mkpd->mkgd", probs, stored[..., head_size:], preferred_element_type=jnp.float32
    )
    mixed = mixed + own_prob.astype(jnp.float32)[..., None] * fresh[:, :, None, head_size:].astype(
        jnp.float32
    )
    return mixed.reshape(items, -1).astype(jnp.bfloat16)


def per_device(
    stream,
    norm_attn,
    norm_ffn,
    w_query,
    w_keyval,
    w_out,
    w_gate,
    w_up,
    w_down,
    cache,
    lengths,
    location,
):
    rows = stream.shape[0]
    resid = stream.astype(jnp.float32)

    own_squares = jnp.sum(resid * resid, axis=1)
    shared = gather_width(jnp.concatenate([own_squares, location.astype(jnp.float32)]))
    squares = jnp.sum(shared[:, :rows], axis=0)
    where = shared[:, rows:].reshape(-1).astype(jnp.int32)
    requests = where.shape[0]
    by_slot = jnp.zeros((requests,), jnp.int32).at[where].set(jnp.arange(requests, dtype=jnp.int32))

    attn_in = scale_rows(resid, squares, norm_attn)
    gathered = lax.all_gather(attn_in, "tensor", axis=0, tiled=True)[by_slot]
    joined = jnp.concatenate(
        [
            jnp.dot(gathered, w_query, preferred_element_type=jnp.float32),
            jnp.dot(gathered, w_keyval, preferred_element_type=jnp.float32),
        ],
        axis=1,
    )
    summed = reduce_rows(joined, WIDTH)
    query_cols = w_query.shape[1]
    query = summed[:, :query_cols].astype(jnp.bfloat16)
    fresh = summed[:, query_cols:].astype(jnp.bfloat16)

    answer = attend(query, fresh, cache, lengths)
    attended = gather_width(answer).reshape(requests, -1)
    mixed = jnp.dot(attended, w_out, preferred_element_type=jnp.float32)[where]
    middle = resid + reduce_rows(mixed, "tensor")

    squares = jnp.sum(gather_width(jnp.sum(middle * middle, axis=1)), axis=0)
    ffn_in = scale_rows(middle, squares, norm_ffn)
    gathered = lax.all_gather(ffn_in, "tensor", axis=0, tiled=True)
    both = lax.psum_scatter(
        jnp.concatenate(
            [
                jnp.dot(gathered, w_gate, preferred_element_type=jnp.float32),
                jnp.dot(gathered, w_up, preferred_element_type=jnp.float32),
            ],
            axis=1,
        ),
        WIDTH,
        scatter_dimension=0,
        tiled=True,
    )
    hidden_cols = w_gate.shape[1]
    hidden = (jax.nn.silu(both[:, :hidden_cols]) * both[:, hidden_cols:]).astype(jnp.bfloat16)
    hidden = lax.all_gather(hidden, WIDTH, axis=0, tiled=True)
    down = jnp.dot(hidden, w_down, preferred_element_type=jnp.float32)
    return middle + reduce_rows(down, "tensor")


def solution(mesh):
    placed = (
        P("tensor", WIDTH),
        P(WIDTH),
        P(WIDTH),
        P(WIDTH, "tensor"),
        P(WIDTH, "tensor"),
        P("tensor", WIDTH),
        P(WIDTH, "tensor"),
        P(WIDTH, "tensor"),
        P("tensor", WIDTH),
        P(WIDTH, "tensor", None, None),
        P(WIDTH),
        P(WIDTH),
    )
    return jax.shard_map(
        per_device,
        mesh=mesh,
        in_specs=placed,
        out_specs=P("tensor", WIDTH),
        check_vma=False,
    )
```

time: 645 us -> 399 us (0.62)
  waiting for transfers between devices: 359 us -> 231 us
  blocking collectives: 198 us -> 84.5 us
  starting transfers between devices: 19 us -> 32.5 us
  matrix products: 20.1 us -> 11.4 us
    psum x2 -> x0, blocking collectives: 142 us -> none  [normed(): squares = lax.psum(jnp.sum(values * values, axis=1), ('group', 'dp'))]
    reduce_scatter x4 -> x1, waiting for transfers between devices: 246 us -> 116 us  [per_device(): lax.psum_scatter(jnp.concatenate([jnp.dot(gathered, w_gate, preferred_ele...]
    all_to_all x3 -> x4, waiting for transfers between devices: 15.1 us -> 63.3 us  [the longest x1 33.9 us: reduce_rows(): return jnp.sum(lax.all_to_all(blocks, axis, 0, 0, tiled=True), axis=0)]
    all_gather x2 -> x1, waiting for transfers between devices: 97.7 us -> 52.3 us  [per_device(): hidden = lax.all_gather(hidden, WIDTH, axis=0, tiled=True)]
    all_to_all x1 -> x2, blocking collectives: 15.9 us -> 43.1 us  [reduce_rows(): return jnp.sum(lax.all_to_all(blocks, axis, 0, 0, tiled=True), axis=0)]
    all_to_all x3 -> x4, starting transfers between devices: 18.8 us -> 32.4 us  [the longest x3 21 us: gather_width(): return lax.all_to_all(sent, WIDTH, 0, 0, tiled=True)]
  transfers between devices with their start and end apart: 9 -> 6, of which waited for: 9 -> 6; matrix products, arithmetic and copies ran while one was open for 2% -> 0% of each run, Pallas kernels for 0% -> 0%
where the time goes in v1:
time: 399 us; the launch traced here: 398 us
  waiting for transfers between devices  231 us (58%)
  blocking collectives  84.5 us (21%)
  starting transfers between devices  32.5 us (8%)
  other arithmetic  15.4 us (4%)
  between operations  13.7 us (3%)
  matrix products  11.4 us (3%)
  local copies, waits for them, and re-layouts  8.85 us (2%)
    reduce_scatter x1, waiting for transfers between devices, per_device(): lax.psum_scatter(jnp.concatenate([jnp.dot(gathered, w_gate, preferred_ele...  116 us
    all_gather x1, waiting for transfers between devices, per_device(): hidden = lax.all_gather(hidden, WIDTH, axis=0, tiled=True)  52.3 us
    all_to_all x2, blocking collectives, reduce_rows(): return jnp.sum(lax.all_to_all(blocks, axis, 0, 0, tiled=True), axis=0)  43.1 us
    all_to_all x1, waiting for transfers between devices, reduce_rows(): return jnp.sum(lax.all_to_all(blocks, axis, 0, 0, tiled=True), axis=0)  33.9 us
    all_to_all x3, waiting for transfers between devices, gather_width(): return lax.all_to_all(sent, WIDTH, 0, 0, tiled=True)  29.4 us
    all_gather x1, blocking collectives, per_device(): gathered = lax.all_gather(attn_in, 'tensor', axis=0, tiled=True)[by_slot]  22.5 us
    all_to_all x3, starting transfers between devices, gather_width(): return lax.all_to_all(sent, WIDTH, 0, 0, tiled=True)  21 us
    all_gather x1, blocking collectives, per_device(): gathered = lax.all_gather(ffn_in, 'tensor', axis=0, tiled=True)  18.9 us
  transfers between devices with their start and end apart: 6, of which 6 were waited for; matrix products, arithmetic and copies ran while one was open for 0% of the time, Pallas kernels for 0%

profile of v1, /device:TPU:1, one launch (start us, length us, event | category | flops | bytes accessed | tf_op | source)
XLA Modules:
  0.0 397.8 jit_solution(13702781530438331024)
XLA Ops:
  6.5 0.0 copy-start
  6.5 0.0 copy-start.4
  6.5 0.0 copy-start.3
  6.5 0.8 convert_element_type.70
  7.3 0.9 fusion.3
  8.2 0.1 pad_maximum_fusion.2
  8.3 0.6 broadcast_in_dim.27
  8.9 8.6 %all-to-all-start = ((f32[32,1,80]{2,1,0:T(1,128)}), f32[32,1,80]{2,1,0:T(1,128)S(1)}, u32[]{:S(2)}, u32[]{:S(2)}) async-start(f32[32,1,80]{2,1,0:T(1,128)} %broadcast_in_dim.27), calls=%async_computation | async-start | bytes 32768 | tf_op jit(solution)/shard_map/all_to_all | solution.py:15
  17.5 0.7 convert_element_type.71
  18.2 6.1 %all-to-all-done = f32[32,1,80]{2,1,0:T(1,128)S(1)} async-done(((f32[32,1,80]{2,1,0:T(1,128)}), f32[32,1,80]{2,1,0:T(1,128)S(1)}, u32[]{:S(2)}, u32[]{:S(2)}) %all-to-all-start) | async-done | bytes 10272 | tf_op jit(solution)/shard_map/all_to_all | solution.py:15
  24.3 0.1 slice_convert_fusion
  24.4 0.1 convert_element_type.74
  24.5 2.4 scatter_custom_fusion
  27.0 0.8 fusion.5
  27.8 22.5 %all_gather.9 = bf16[512,256]{1,0:T(8,128)(2,1)S(1)} all-gather(bf16[64,256]{1,0:T(8,128)(2,1)S(1)} %fusion.5), channel_id=1, replica_groups=mesh['group'=2,'dp'=16,'tensor'=8] {'tensor'}, dimensions={0}, use_global_device_ids=true | all-gather | bytes 294912 | tf_op jit(solution)/shard_map/all_gather | solution.py:90
  50.4 1.9 gather_fusion
  52.3 0.0 copy-done.4
  52.3 0.2 fusion.20
  52.6 0.0 copy-done.3
  52.6 0.4 fusion.19
  53.0 1.7 pad_maximum_fusion.1
  54.7 0.0 copy-start.5
  54.7 11.4 %all-to-all-start.1 = ((f32[32,16,1280]{2,1,0:T(8,128)}), f32[32,16,1280]{2,1,0:T(8,128)}, u32[]{:S(2)}, u32[]{:S(2)}) async-start(f32[32,16,1280]{2,1,0:T(8,128)} %bitcast.51), calls=%async_computation.1 | async-start | bytes 5242880 | tf_op jit(solution)/shard_map/all_to_all | solution.py:26
  66.2 0.0 copy-done.5
  66.2 0.1 iota_compare_fusion
  66.3 33.9 %all-to-all-done.1 = f32[32,16,1280]{2,1,0:T(8,128)} async-done(((f32[32,16,1280]{2,1,0:T(8,128)}), f32[32,16,1280]{2,1,0:T(8,128)}, u32[]{:S(2)}, u32[]{:S(2)}) %all-to-all-start.1) | async-done | bytes 2621472 | tf_op jit(solution)/shard_map/all_to_all | solution.py:26
  100.1 1.9 reduce_sum.74
  102.0 0.1 fusion.11
  102.2 1.7 select_reduce_fusion
  103.9 0.2 fusion.2
  104.1 1.5 fusion
  105.6 1.1 broadcast_in_dim.31
  106.8 5.2 %all-to-all-start.2 = ((bf16[32,16,1024]{2,1,0:T(8,128)(2,1)}), bf16[32,16,1024]{2,1,0:T(8,128)(2,1)S(1)}, u32[]{:S(2)}, u32[]{:S(2)}) async-start(bf16[32,16,1024]{2,1,0:T(8,128)(2,1)} %broadcast_in_dim.31), calls=%async_computation.2 | async-start | bytes 2097152 | tf_op jit(solution)/shard_map/all_to_all | solution.py:15
  111.9 16.5 %all-to-all-done.2 = bf16[32,16,1024]{2,1,0:T(8,128)(2,1)S(1)} async-done(((bf16[32,16,1024]{2,1,0:T(8,128)(2,1)}), bf16[32,16,1024]{2,1,0:T(8,128)(2,1)S(1)}, u32[]{:S(2)}, u32[]{:S(2)}) %all-to-all-start.2) | async-done | bytes 1048608 | tf_op jit(solution)/shard_map/all_to_all | solution.py:15
  128.5 1.5 fusion.21
  130.0 0.0 copy-start.2
  130.0 0.0 copy-start.6
  130.0 1.6 gather_fusion.1
  131.6 19.2 %all_to_all.35 = f32[8,64,256]{2,1,0:T(8,128)S(1)} all-to-all(f32[8,64,256]{2,1,0:T(8,128)S(1)} %bitcast.53), channel_id=1, replica_groups=mesh['group'=2,'dp'=16,'tensor'=8] {'tensor'}, dimensions={0} | all-to-all | bytes 1048576 | tf_op jit(solution)/shard_map/all_to_all | solution.py:26
  150.8 0.0 copy-done.2
  150.9 0.1 multiply_reduce_fusion
  151.0 0.6 broadcast_in_dim.32
  151.6 7.2 %all-to-all-start.4 = ((f32[32,1,64]{2,1,0:T(1,128)}), f32[32,1,64]{2,1,0:T(1,128)S(1)}, u32[]{:S(2)}, u32[]{:S(2)}) async-start(f32[32,1,64]{2,1,0:T(1,128)} %broadcast_in_dim.32), calls=%async_computation.4 | async-start | bytes 32768 | tf_op jit(solution)/shard_map/all_to_all | solution.py:15
  158.9 0.0 reduce-scatter.2.cloned.1.call-start
  158.9 0.0 copy-done.6
  158.9 6.7 %all-to-all-done.4 = f32[32,1,64]{2,1,0:T(1,128)S(1)} async-done(((f32[32,1,64]{2,1,0:T(1,128)}), f32[32,1,64]{2,1,0:T(1,128)S(1)}, u32[]{:S(2)}, u32[]{:S(2)}) %all-to-all-start.4) | async-done | bytes 8224 | tf_op jit(solution)/shard_map/all_to_all | solution.py:15
  165.7 0.1 multiply_convert_fusion
  165.8 18.9 %all_gather.10 = bf16[512,256]{1,0:T(8,128)(2,1)S(1)} all-gather(bf16[64,256]{1,0:T(8,128)(2,1)S(1)} %multiply_convert_fusion), channel_id=1, replica_groups=mesh['group'=2,'dp'=16,'tensor'=8] {'tensor'}, dimensions={0}, use_global_device_ids=true | all-gather | bytes 294912 | tf_op jit(solution)/shard_map/all_gather | solution.py:110
  184.7 0.0 copy-done
  184.7 0.0 copy-start.1
  184.7 1.1 fusion.23
  185.8 0.4 copy-done.1
  186.2 1.1 fusion.22
  187.3 5.5 %pad_maximum_fusion = f32[512,7168]{1,0:T(8,128)} fusion(f32[512,3584]{1,0:T(8,128)S(1)} %fusion.23, f32[512,3584]{1,0:T(8,128)S(1)} %fusion.22), kind=kLoop, calls=%fused_computation.3 | loop fusion | flops 3670016 | bytes 29360128 | tf_op jit(solution)/shard_map/concatenate | solution.py:112
  192.8 0.0 reduce-scatter.2.cloned.1.call-update
  192.8 0.0 all-gather.2.cloned.1.call-start
  192.8 115.8 %reduce-scatter.2.cloned.1.call-done = f32[16,7168]{1,0:T(8,128)} async-done(((f32[512,7168]{1,0:T(8,128)}), f32[16,7168]{1,0:T(8,128)}) %reduce-scatter.2.cloned.1.call-update) | async-done | bytes 458768 | tf_op jit(solution)/shard_map/reduce_scatter | solution.py:111
  308.6 1.8 fusion.1
  310.4 0.0 all-gather.2.cloned.1.call-update
  310.4 52.3 %all-gather.2.cloned.1.call-done = bf16[512,3584]{1,0:T(8,128)(2,1)} async-done(((bf16[16,3584]{1,0:T(8,128)(2,1)}), bf16[512,3584]{1,0:T(8,128)(2,1)}) %all-gather.2.cloned.1.call-update) | async-done | bytes 3670032 | tf_op jit(solution)/shard_map/all_gather | solution.py:125
  362.7 3.7 fusion.24
  366.4 23.9 %all_to_all.36 = f32[8,64,256]{2,1,0:T(8,128)S(1)} all-to-all(f32[8,64,256]{2,1,0:T(8,128)S(1)} %bitcast.56), channel_id=1, replica_groups=mesh['group'=2,'dp'=16,'tensor'=8] {'tensor'}, dimensions={0} | all-to-all | bytes 1048576 | tf_op jit(solution)/shard_map/all_to_all | solution.py:26
  390.3 0.6 fusion.10
  (19 shorter events, 0.2 us)
Async XLA Ops:
  6.5 178.1 %copy-start = (bf16[256,3584]{1,0:T(8,128)(2,1)S(1)}, bf16[256,3584]{1,0:T(8,128)(2,1)}, u32[]{:S(2)}) copy-start(bf16[256,3584]{1,0:T(8,128)(2,1)} %param.19) | copy-start | bytes 5505028
  6.5 45.8 %copy-start.4 = (bf16[256,256]{1,0:T(8,128)(2,1)S(1)}, bf16[256,256]{1,0:T(8,128)(2,1)}, u32[]{:S(2)}) copy-start(bf16[256,256]{1,0:T(8,128)(2,1)} %param.16) | copy-start | bytes 393220
  6.5 46.0 %copy-start.3 = (bf16[256,1024]{1,0:T(8,128)(2,1)S(1)}, bf16[256,1024]{1,0:T(8,128)(2,1)}, u32[]{:S(2)}) copy-start(bf16[256,1024]{1,0:T(8,128)(2,1)} %param.15) | copy-start | bytes 1572868
  8.9 15.4 %all-to-all-start = ((f32[32,1,80]{2,1,0:T(1,128)}), f32[32,1,80]{2,1,0:T(1,128)S(1)}, u32[]{:S(2)}, u32[]{:S(2)}) async-start(f32[32,1,80]{2,1,0:T(1,128)} %broadcast_in_dim.27), calls=%async_computation | async-start | bytes 32768 | tf_op jit(solution)/shard_map/all_to_all | solution.py:15
  54.7 11.4 %copy-start.5 = (s32[16]{0:T(128)S(1)}, s32[16]{0:T(128)}, u32[]{:S(2)}) copy-start(s32[16]{0:T(128)} %param.22) | copy-start | bytes 196
  54.7 45.4 %all-to-all-start.1 = ((f32[32,16,1280]{2,1,0:T(8,128)}), f32[32,16,1280]{2,1,0:T(8,128)}, u32[]{:S(2)}, u32[]{:S(2)}) async-start(f32[32,16,1280]{2,1,0:T(8,128)} %bitcast.51), calls=%async_computation.1 | async-start | bytes 5242880 | tf_op jit(solution)/shard_map/all_to_all | solution.py:26
  106.8 21.7 %all-to-all-start.2 = ((bf16[32,16,1024]{2,1,0:T(8,128)(2,1)}), bf16[32,16,1024]{2,1,0:T(8,128)(2,1)S(1)}, u32[]{:S(2)}, u32[]{:S(2)}) async-start(bf16[32,16,1024]{2,1,0:T(8,128)(2,1)} %broadcast_in_dim.31), calls=%async_computation.2 | async-start | bytes 2097152 | tf_op jit(solution)/shard_map/all_to_all | solution.py:15
  130.0 20.9 %copy-start.2 = (bf16[64,256]{1,0:T(8,128)(2,1)S(1)}, bf16[64,256]{1,0:T(8,128)(2,1)}, u32[]{:S(2)}) copy-start(bf16[64,256]{1,0:T(8,128)(2,1)} %param.12) | copy-start | bytes 98308
  130.0 28.9 %copy-start.6 = (bf16[256]{0:T(256)(128)(2,1)S(1)}, bf16[256]{0:T(256)(128)(2,1)}, u32[]{:S(2)}) copy-start(bf16[256]{0:T(256)(128)(2,1)} %param.14) | copy-start | bytes 1540
  151.6 14.1 %all-to-all-start.4 = ((f32[32,1,64]{2,1,0:T(1,128)}), f32[32,1,64]{2,1,0:T(1,128)S(1)}, u32[]{:S(2)}, u32[]{:S(2)}) async-start(f32[32,1,64]{2,1,0:T(1,128)} %broadcast_in_dim.32), calls=%async_computation.4 | async-start | bytes 32768 | tf_op jit(solution)/shard_map/all_to_all | solution.py:15
  158.9 149.8 %reduce-scatter.2.cloned.1.call-start = ((), (), s32[]{:S(2)}) async-start(), calls=%async_computation.7 | async-start | bytes 15138816 | tf_op jit(solution)/shard_map/reduce_scatter | solution.py:111
  184.7 1.5 copy-start.1
  192.8 169.9 %all-gather.2.cloned.1.call-start = ((), (), s32[]{:S(2)}) async-start(), calls=%async_computation.8 | async-start | bytes 3784704 | tf_op jit(solution)/shard_map/all_gather | solution.py:125
Sparse Core Ops, SparseCore 0:
  192.9 115.6 reduce-scatter.1
  311.2 51.4 all-gather.1

commit v2 on v1

--- a/solution.py
+++ b/solution.py
@@ -18,6 +18,24 @@
 def scale_rows(values, squares, gain):
     scale = lax.rsqrt(squares / D + EPSILON)
     return (values * scale[:, None] * gain.astype(jnp.float32)[None, :]).astype(jnp.bfloat16)
+
+
+def gather_rows(values):
+    chips = lax.axis_size("dp")
+    across = lax.all_to_all(
+        jnp.broadcast_to(values[None], (chips,) + values.shape), "dp", 0, 0, tiled=True
+    )
+    both = lax.all_gather(across, "group", axis=0, tiled=True)
+    return both.reshape((-1,) + values.shape[1:])
+
+
+def reduce_width(partial, link_type):
+    cores = lax.axis_size("group")
+    chips = lax.axis_size("dp")
+    blocks = partial.reshape((cores, chips, partial.shape[0] // (cores * chips)) + partial.shape[1:])
+    on_chip = jnp.sum(lax.all_to_all(blocks, "group", 0, 0, tiled=True), axis=0)
+    moved = lax.all_to_all(on_chip.astype(link_type), "dp", 0, 0, tiled=True)
+    return jnp.sum(moved.astype(jnp.float32), axis=0)
 
 
 def reduce_rows(partial, axis):
@@ -95,20 +113,20 @@
         ],
         axis=1,
     )
-    summed = reduce_rows(joined, WIDTH)
+    summed = reduce_width(joined, jnp.float32)
     query_cols = w_query.shape[1]
     query = summed[:, :query_cols].astype(jnp.bfloat16)
     fresh = summed[:, query_cols:].astype(jnp.bfloat16)
 
     answer = attend(query, fresh, cache, lengths)
-    attended = gather_width(answer).reshape(requests, -1)
+    attended = gather_rows(answer)
     mixed = jnp.dot(attended, w_out, preferred_element_type=jnp.float32)[where]
     middle = resid + reduce_rows(mixed, "tensor")
 
     squares = jnp.sum(gather_width(jnp.sum(middle * middle, axis=1)), axis=0)
     ffn_in = scale_rows(middle, squares, norm_ffn)
     gathered = lax.all_gather(ffn_in, "tensor", axis=0, tiled=True)
-    both = lax.psum_scatter(
+    both = reduce_width(
         jnp.concatenate(
             [
                 jnp.dot(gathered, w_gate, preferred_element_type=jnp.float32),
@@ -116,13 +134,11 @@
             ],
             axis=1,
         ),
-        WIDTH,
-        scatter_dimension=0,
-        tiled=True,
+        jnp.bfloat16,
     )
     hidden_cols = w_gate.shape[1]
     hidden = (jax.nn.silu(both[:, :hidden_cols]) * both[:, hidden_cols:]).astype(jnp.bfloat16)
-    hidden = lax.all_gather(hidden, WIDTH, axis=0, tiled=True)
+    hidden = gather_rows(hidden)
     down = jnp.dot(hidden, w_down, preferred_element_type=jnp.float32)
     return middle + reduce_rows(down, "tensor")
 

time: 399 us -> 350 us (0.88)
  waiting for transfers between devices: 231 us -> 60.1 us
  blocking collectives: 84.5 us -> 216 us
  starting transfers between devices: 32.5 us -> 19.9 us
    all_to_all x0 -> x5, blocking collectives: none -> 127 us  [the longest x1 48.6 us: reduce_width(): moved = lax.all_to_all(on_chip.astype(link_type), 'dp', 0, 0, tiled=True)]
    reduce_scatter x1 -> x0, waiting for transfers between devices: 116 us -> none  [per_device(): lax.psum_scatter(jnp.concatenate([jnp.dot(gathered, w_gate, preferred_ele...]
    all_gather x1 -> x2, waiting for transfers between devices: 52.3 us -> 26.1 us  [gather_rows(): both = lax.all_gather(across, 'group', axis=0, tiled=True)]
    all_to_all x3 -> x2, waiting for transfers between devices: 29.4 us -> 12.9 us  [gather_width(): return lax.all_to_all(sent, WIDTH, 0, 0, tiled=True)]
    reduce_sum x0 -> x4, other arithmetic: none -> 12.9 us  [the longest x2 12.3 us: reduce_width(): on_chip = jnp.sum(lax.all_to_all(blocks, 'group', 0, 0, tiled=True), axis=0)]
    all_to_all x1, waiting for transfers between devices: 33.9 us -> 21.1 us  [reduce_width(): moved = lax.all_to_all(on_chip.astype(link_type), 'dp', 0, 0, tiled=True)]
    all_to_all x1, starting transfers between devices: 11.4 us -> 3.7 us  [reduce_width(): moved = lax.all_to_all(on_chip.astype(link_type), 'dp', 0, 0, tiled=True)]
    all_to_all x2, blocking collectives: 43.1 us -> 48.1 us  [reduce_rows(): return jnp.sum(lax.all_to_all(blocks, axis, 0, 0, tiled=True), axis=0)]
  transfers between devices with their start and end apart: 6 -> 5, of which waited for: 6 -> 5; matrix products, arithmetic and copies ran while one was open for 0% -> 0% of each run, Pallas kernels for 0% -> 0%
where the time goes in v2:
time: 350 us; the launch traced here: 349 us
  blocking collectives  216 us (62%)
  waiting for transfers between devices  60.1 us (17%)
  starting transfers between devices  19.9 us (6%)
  other arithmetic  19.1 us (5%)
  between operations  13.7 us (4%)
  matrix products  11.8 us (3%)
  local copies, waits for them, and re-layouts  7.96 us (2%)
    all_to_all x1, blocking collectives, reduce_width(): moved = lax.all_to_all(on_chip.astype(link_type), 'dp', 0, 0, tiled=True)  48.6 us
    all_to_all x2, blocking collectives, reduce_rows(): return jnp.sum(lax.all_to_all(blocks, axis, 0, 0, tiled=True), axis=0)  48.1 us
    all_to_all x2, blocking collectives, gather_rows(): lax.all_to_all(jnp.broadcast_to(values[None], (chips,) + values.shape), '...  41.3 us
    all_to_all x2, blocking collectives, reduce_width(): on_chip = jnp.sum(lax.all_to_all(blocks, 'group', 0, 0, tiled=True), axis=0)  36.9 us
    all_gather x2, waiting for transfers between devices, gather_rows(): both = lax.all_gather(across, 'group', axis=0, tiled=True)  26.1 us
    all_gather x1, blocking collectives, per_device(): gathered = lax.all_gather(attn_in, 'tensor', axis=0, tiled=True)[by_slot]  22.5 us
    all_to_all x1, waiting for transfers between devices, reduce_width(): moved = lax.all_to_all(on_chip.astype(link_type), 'dp', 0, 0, tiled=True)  21.1 us
    all_gather x1, blocking collectives, per_device(): gathered = lax.all_gather(ffn_in, 'tensor', axis=0, tiled=True)  18.9 us
  transfers between devices with their start and end apart: 5, of which 5 were waited for; matrix products, arithmetic and copies ran while one was open for 0% of the time, Pallas kernels for 0%

profile of v2, /device:TPU:1, one launch (start us, length us, event | category | flops | bytes accessed | tf_op | source)
XLA Modules:
  0.0 349.0 jit_solution(18218237852078352862)
XLA Ops:
  6.5 0.0 copy-start
  6.5 0.8 convert_element_type.76
  7.3 0.9 fusion.5
  8.2 0.1 pad_maximum_fusion.2
  8.3 0.6 broadcast_in_dim.29
  8.9 8.6 %all-to-all-start = ((f32[32,1,80]{2,1,0:T(1,128)}), f32[32,1,80]{2,1,0:T(1,128)S(1)}, u32[]{:S(2)}, u32[]{:S(2)}) async-start(f32[32,1,80]{2,1,0:T(1,128)} %broadcast_in_dim.29), calls=%async_computation | async-start | bytes 32768 | tf_op jit(solution)/shard_map/all_to_all | solution.py:15
  17.5 0.7 convert_element_type.77
  18.2 6.1 %all-to-all-done = f32[32,1,80]{2,1,0:T(1,128)S(1)} async-done(((f32[32,1,80]{2,1,0:T(1,128)}), f32[32,1,80]{2,1,0:T(1,128)S(1)}, u32[]{:S(2)}, u32[]{:S(2)}) %all-to-all-start) | async-done | bytes 10272 | tf_op jit(solution)/shard_map/all_to_all | solution.py:15
  24.3 0.1 slice_convert_fusion
  24.4 0.1 convert_element_type.80
  24.5 2.4 scatter_custom_fusion
  27.0 0.8 fusion.7
  27.8 22.5 %all_gather.12 = bf16[512,256]{1,0:T(8,128)(2,1)S(1)} all-gather(bf16[64,256]{1,0:T(8,128)(2,1)S(1)} %fusion.7), channel_id=1, replica_groups=mesh['group'=2,'dp'=16,'tensor'=8] {'tensor'}, dimensions={0}, use_global_device_ids=true | all-gather | bytes 294912 | tf_op jit(solution)/shard_map/all_gather | solution.py:108
  50.4 1.9 gather_fusion
  52.3 0.0 copy-done.6
  52.3 0.2 fusion.22
  52.6 0.0 copy-done.4
  52.6 0.4 fusion.21
  53.0 0.2 pad_maximum_fusion.1
  53.2 13.2 %all_to_all.55 = f32[2,16,16,1280]{3,2,1,0:T(8,128)} all-to-all(f32[2,16,16,1280]{3,2,1,0:T(8,128)S(1)} %bitcast.55), channel_id=1, replica_groups=mesh['group'=2,'dp'=16,'tensor'=8] {'group'}, dimensions={0} | all-to-all | bytes 5242880 | tf_op jit(solution)/shard_map/all_to_all | solution.py:36
  66.4 3.1 reduce_sum.101
  69.5 3.7 %all-to-all-start.2 = ((f32[16,16,1280]{2,1,0:T(8,128)}), f32[16,16,1280]{2,1,0:T(8,128)S(1)}, u32[]{:S(2)}, u32[]{:S(2)}) async-start(f32[16,16,1280]{2,1,0:T(8,128)} %reduce_sum.101), calls=%async_computation.2 | async-start | bytes 2621440 | tf_op jit(solution)/shard_map/all_to_all | solution.py:37
  73.2 0.0 all-gather.3.cloned.1.call-start
  73.3 0.0 copy-done.7
  73.3 0.1 iota_compare_fusion
  73.4 21.1 %all-to-all-done.2 = f32[16,16,1280]{2,1,0:T(8,128)S(1)} async-done(((f32[16,16,1280]{2,1,0:T(8,128)}), f32[16,16,1280]{2,1,0:T(8,128)S(1)}, u32[]{:S(2)}, u32[]{:S(2)}) %all-to-all-start.2) | async-done | bytes 1310752 | tf_op jit(solution)/shard_map/all_to_all | solution.py:37
  94.5 0.1 reduce_sum.102
  94.6 0.1 fusion.13
  94.8 1.8 select_reduce_fusion
  96.5 0.2 fusion.4
  96.7 1.5 fusion.2
  98.3 0.1 broadcast_in_dim.33
  98.4 13.9 %all_to_all.56 = bf16[16,16,1024]{2,1,0:T(8,128)(2,1)} all-to-all(bf16[16,16,1024]{2,1,0:T(8,128)(2,1)S(1)} %broadcast_in_dim.33), channel_id=1, replica_groups=mesh['group'=2,'dp'=16,'tensor'=8] {'dp'}, dimensions={0} | all-to-all | bytes 1048576 | tf_op jit(solution)/shard_map/all_to_all | solution.py:25
  112.3 0.0 all-gather.3.cloned.1.call-update
  112.3 11.8 %all-gather.3.cloned.1.call-done = bf16[32,16,1024]{2,1,0:T(8,128)(2,1)} async-done(((bf16[16,16,1024]{2,1,0:T(8,128)(2,1)}), bf16[32,16,1024]{2,1,0:T(8,128)(2,1)}) %all-gather.3.cloned.1.call-update) | async-done | bytes 1048592 | tf_op jit(solution)/shard_map/all_gather | solution.py:28
  124.1 0.0 copy-done.5
  124.1 1.7 fusion.23
  125.8 0.0 copy-start.3
  125.8 0.0 copy-start.8
  125.8 1.6 gather_fusion.1
  127.4 24.1 %all_to_all.57 = f32[8,64,256]{2,1,0:T(8,128)S(1)} all-to-all(f32[8,64,256]{2,1,0:T(8,128)S(1)} %bitcast.56), channel_id=1, replica_groups=mesh['group'=2,'dp'=16,'tensor'=8] {'tensor'}, dimensions={0} | all-to-all | bytes 1048576 | tf_op jit(solution)/shard_map/all_to_all | solution.py:44
  151.5 0.1 multiply_reduce_fusion
  151.6 0.6 broadcast_in_dim.34
  152.2 7.5 %all-to-all-start.5 = ((f32[32,1,64]{2,1,0:T(1,128)}), f32[32,1,64]{2,1,0:T(1,128)S(1)}, u32[]{:S(2)}, u32[]{:S(2)}) async-start(f32[32,1,64]{2,1,0:T(1,128)} %broadcast_in_dim.34), calls=%async_computation.5 | async-start | bytes 32768 | tf_op jit(solution)/shard_map/all_to_all | solution.py:15
  159.7 0.0 all-gather.5.cloned.1.call-start
  159.8 6.7 %all-to-all-done.5 = f32[32,1,64]{2,1,0:T(1,128)S(1)} async-done(((f32[32,1,64]{2,1,0:T(1,128)}), f32[32,1,64]{2,1,0:T(1,128)S(1)}, u32[]{:S(2)}, u32[]{:S(2)}) %all-to-all-start.5) | async-done | bytes 8224 | tf_op jit(solution)/shard_map/all_to_all | solution.py:15
  166.6 0.1 multiply_convert_fusion
  166.7 18.9 %all_gather.14 = bf16[512,256]{1,0:T(8,128)(2,1)S(1)} all-gather(bf16[64,256]{1,0:T(8,128)(2,1)S(1)} %multiply_convert_fusion), channel_id=1, replica_groups=mesh['group'=2,'dp'=16,'tensor'=8] {'tensor'}, dimensions={0}, use_global_device_ids=true | all-gather | bytes 294912 | tf_op jit(solution)/shard_map/all_gather | solution.py:128
  185.5 1.1 fusion.25
  186.7 0.4 copy-done.2
  187.0 1.1 fusion.24
  188.2 1.3 pad_maximum_fusion
  189.5 23.7 %all_to_all.58 = f32[2,16,16,7168]{3,2,1,0:T(8,128)} all-to-all(f32[2,16,16,7168]{3,2,1,0:T(8,128)S(1)} %bitcast.54), channel_id=1, replica_groups=mesh['group'=2,'dp'=16,'tensor'=8] {'group'}, dimensions={0} | all-to-all | bytes 29360128 | tf_op jit(solution)/shard_map/all_to_all | solution.py:36
  213.2 9.2 %reduce_sum.107 = bf16[16,16,7168]{2,1,0:T(8,128)(2,1)} reduce(f32[2,16,16,7168]{3,2,1,0:T(8,128)} %all_to_all.58, f32[]{:T(128)} %constant.9.clone.1), dimensions={0}, to_apply=%region_10.11 | reduce | flops 1835008 | bytes 18350084 | tf_op jit(solution)/shard_map/reduce_sum | solution.py:36
  222.4 48.6 %all_to_all.59 = bf16[16,16,7168]{2,1,0:T(8,128)(2,1)S(1)} all-to-all(bf16[16,16,7168]{2,1,0:T(8,128)(2,1)} %reduce_sum.107), channel_id=1, replica_groups=mesh['group'=2,'dp'=16,'tensor'=8] {'dp'}, dimensions={0} | all-to-all | bytes 7340032 | tf_op jit(solution)/shard_map/all_to_all | solution.py:37
  271.0 0.5 convert_reduce_fusion
  271.6 0.1 fusion.3
  271.6 0.2 broadcast_in_dim.35
  271.8 27.4 %all_to_all.60 = bf16[16,16,3584]{2,1,0:T(8,128)(2,1)} all-to-all(bf16[16,16,3584]{2,1,0:T(8,128)(2,1)S(1)} %broadcast_in_dim.35), channel_id=1, replica_groups=mesh['group'=2,'dp'=16,'tensor'=8] {'dp'}, dimensions={0} | all-to-all | bytes 3670016 | tf_op jit(solution)/shard_map/all_to_all | solution.py:25
  299.2 0.0 all-gather.5.cloned.1.call-update
  299.2 14.3 %all-gather.5.cloned.1.call-done = bf16[32,16,3584]{2,1,0:T(8,128)(2,1)} async-done(((bf16[16,16,3584]{2,1,0:T(8,128)(2,1)}), bf16[32,16,3584]{2,1,0:T(8,128)(2,1)}) %all-gather.5.cloned.1.call-update) | async-done | bytes 3670032 | tf_op jit(solution)/shard_map/all_gather | solution.py:28
  313.6 3.8 %fusion = f32[8,64,256]{2,1,0:T(8,128)S(1)} fusion(bf16[8,64,3584]{2,1,0:T(8,128)(2,1)} %bitcast.71, bf16[3584,256]{1,0:T(8,128)(2,1)} %param.20), kind=kOutput, calls=%fused_computation.6 | convolution fusion | flops 939524096 | bytes 6029312 | tf_op jit(solution)/shard_map/dot_general | solution.py:142
  317.4 24.1 %all_to_all.61 = f32[8,64,256]{2,1,0:T(8,128)S(1)} all-to-all(f32[8,64,256]{2,1,0:T(8,128)S(1)} %fusion), channel_id=1, replica_groups=mesh['group'=2,'dp'=16,'tensor'=8] {'tensor'}, dimensions={0} | all-to-all | bytes 1048576 | tf_op jit(solution)/shard_map/all_to_all | solution.py:44
  341.5 0.6 fusion.12
  (29 shorter events, 0.2 us)
Async XLA Ops:
  6.5 179.0 %copy-start = (bf16[256,3584]{1,0:T(8,128)(2,1)S(1)}, bf16[256,3584]{1,0:T(8,128)(2,1)}, u32[]{:S(2)}) copy-start(bf16[256,3584]{1,0:T(8,128)(2,1)} %param.19) | copy-start | bytes 5505028
  6.5 45.8 %copy-start.6 = (bf16[256,256]{1,0:T(8,128)(2,1)S(1)}, bf16[256,256]{1,0:T(8,128)(2,1)}, u32[]{:S(2)}) copy-start(bf16[256,256]{1,0:T(8,128)(2,1)} %param.16) | copy-start | bytes 393220
  6.5 46.0 %copy-start.4 = (bf16[256,1024]{1,0:T(8,128)(2,1)S(1)}, bf16[256,1024]{1,0:T(8,128)(2,1)}, u32[]{:S(2)}) copy-start(bf16[256,1024]{1,0:T(8,128)(2,1)} %param.15) | copy-start | bytes 1572868
  8.9 15.4 %all-to-all-start = ((f32[32,1,80]{2,1,0:T(1,128)}), f32[32,1,80]{2,1,0:T(1,128)S(1)}, u32[]{:S(2)}, u32[]{:S(2)}) async-start(f32[32,1,80]{2,1,0:T(1,128)} %broadcast_in_dim.29), calls=%async_computation | async-start | bytes 32768 | tf_op jit(solution)/shard_map/all_to_all | solution.py:15
  66.4 6.9 %copy-start.7 = (s32[16]{0:T(128)S(1)}, s32[16]{0:T(128)}, u32[]{:S(2)}) copy-start(s32[16]{0:T(128)} %param.22) | copy-start | bytes 196
  69.5 25.0 %all-to-all-start.2 = ((f32[16,16,1280]{2,1,0:T(8,128)}), f32[16,16,1280]{2,1,0:T(8,128)S(1)}, u32[]{:S(2)}, u32[]{:S(2)}) async-start(f32[16,16,1280]{2,1,0:T(8,128)} %reduce_sum.101), calls=%async_computation.2 | async-start | bytes 2621440 | tf_op jit(solution)/shard_map/all_to_all | solution.py:37
  73.2 50.8 %all-gather.3.cloned.1.call-start = ((), (), s32[]{:S(2)}) async-start(), calls=%async_computation.10 | async-start | bytes 1572864 | tf_op jit(solution)/shard_map/all_gather | solution.py:28
  94.8 29.3 %copy-start.5 = (bf16[1024,256]{1,0:T(8,128)(2,1)S(1)}, bf16[1024,256]{1,0:T(8,128)(2,1)}, u32[]{:S(2)}) copy-start(bf16[1024,256]{1,0:T(8,128)(2,1)} %param.17) | copy-start | bytes 1572868
  125.8 25.7 %copy-start.3 = (bf16[64,256]{1,0:T(8,128)(2,1)S(1)}, bf16[64,256]{1,0:T(8,128)(2,1)}, u32[]{:S(2)}) copy-start(bf16[64,256]{1,0:T(8,128)(2,1)} %param.12) | copy-start | bytes 98308
  125.8 34.0 %copy-start.8 = (bf16[256]{0:T(256)(128)(2,1)S(1)}, bf16[256]{0:T(256)(128)(2,1)}, u32[]{:S(2)}) copy-start(bf16[256]{0:T(256)(128)(2,1)} %param.14) | copy-start | bytes 1540
  152.2 14.3 %all-to-all-start.5 = ((f32[32,1,64]{2,1,0:T(1,128)}), f32[32,1,64]{2,1,0:T(1,128)S(1)}, u32[]{:S(2)}, u32[]{:S(2)}) async-start(f32[32,1,64]{2,1,0:T(1,128)} %broadcast_in_dim.34), calls=%async_computation.5 | async-start | bytes 32768 | tf_op jit(solution)/shard_map/all_to_all | solution.py:15
  159.7 153.8 %all-gather.5.cloned.1.call-start = ((), (), s32[]{:S(2)}) async-start(), calls=%async_computation.11 | async-start | bytes 5505024 | tf_op jit(solution)/shard_map/all_gather | solution.py:28
  185.5 1.5 copy-start.2
  313.6 28.6 %copy-start.1 = (bf16[256,3584]{1,0:T(8,128)(2,1)S(1)}, bf16[256,3584]{1,0:T(8,128)(2,1)}, u32[]{:S(2)}) copy-start(bf16[256,3584]{1,0:T(8,128)(2,1)} %param.19) | copy-start | bytes 5505028
Sparse Core Ops, SparseCore 0:
  112.4 11.5 all-gather.2
  299.3 14.1 all-gather.4

commit v3 on v2

--- a/solution.py
+++ b/solution.py
@@ -29,13 +29,24 @@
     return both.reshape((-1,) + values.shape[1:])
 
 
-def reduce_width(partial, link_type):
+def reduce_chips(partial, link_type):
+    chips = lax.axis_size("dp")
+    blocks = partial.reshape((chips, partial.shape[0] // chips) + partial.shape[1:])
+    moved = lax.all_to_all(blocks.astype(link_type), "dp", 0, 0, tiled=True)
+    return jnp.sum(moved.astype(jnp.float32), axis=0)
+
+
+def chip_rows(values):
+    both = lax.all_gather(values, ("group", "tensor"), axis=0, tiled=True)
     cores = lax.axis_size("group")
-    chips = lax.axis_size("dp")
-    blocks = partial.reshape((cores, chips, partial.shape[0] // (cores * chips)) + partial.shape[1:])
-    on_chip = jnp.sum(lax.all_to_all(blocks, "group", 0, 0, tiled=True), axis=0)
-    moved = lax.all_to_all(on_chip.astype(link_type), "dp", 0, 0, tiled=True)
-    return jnp.sum(moved.astype(jnp.float32), axis=0)
+    parts = lax.axis_size("tensor")
+    rows, width = values.shape
+    both = both.reshape(cores, parts, rows, width).transpose(1, 2, 0, 3)
+    return both.reshape(parts * rows, cores * width)
+
+
+def chip_weights(matrices):
+    return lax.all_gather(jnp.concatenate(matrices, axis=1), "group", axis=0, tiled=True)
 
 
 def reduce_rows(partial, axis):
@@ -104,16 +115,16 @@
     requests = where.shape[0]
     by_slot = jnp.zeros((requests,), jnp.int32).at[where].set(jnp.arange(requests, dtype=jnp.int32))
 
+    core = lax.axis_index("group")
+    half = requests // lax.axis_size("group")
+    qkv_weights = chip_weights((w_query, w_keyval))
+    ffn_weights = chip_weights((w_gate, w_up))
+
     attn_in = scale_rows(resid, squares, norm_attn)
-    gathered = lax.all_gather(attn_in, "tensor", axis=0, tiled=True)[by_slot]
-    joined = jnp.concatenate(
-        [
-            jnp.dot(gathered, w_query, preferred_element_type=jnp.float32),
-            jnp.dot(gathered, w_keyval, preferred_element_type=jnp.float32),
-        ],
-        axis=1,
-    )
-    summed = reduce_width(joined, jnp.float32)
+    mine = lax.dynamic_slice_in_dim(by_slot, core * half, half)
+    gathered = chip_rows(attn_in)[mine]
+    joined = jnp.dot(gathered, qkv_weights, preferred_element_type=jnp.float32)
+    summed = reduce_chips(joined, jnp.float32)
     query_cols = w_query.shape[1]
     query = summed[:, :query_cols].astype(jnp.bfloat16)
     fresh = summed[:, query_cols:].astype(jnp.bfloat16)
@@ -125,16 +136,9 @@
 
     squares = jnp.sum(gather_width(jnp.sum(middle * middle, axis=1)), axis=0)
     ffn_in = scale_rows(middle, squares, norm_ffn)
-    gathered = lax.all_gather(ffn_in, "tensor", axis=0, tiled=True)
-    both = reduce_width(
-        jnp.concatenate(
-            [
-                jnp.dot(gathered, w_gate, preferred_element_type=jnp.float32),
-                jnp.dot(gathered, w_up, preferred_element_type=jnp.float32),
-            ],
-            axis=1,
-        ),
-        jnp.bfloat16,
+    gathered = lax.dynamic_slice_in_dim(chip_rows(ffn_in), core * half, half)
+    both = reduce_chips(
+        jnp.dot(gathered, ffn_weights, preferred_element_type=jnp.float32), jnp.bfloat16
     )
     hidden_cols = w_gate.shape[1]
     hidden = (jax.nn.silu(both[:, :hidden_cols]) * both[:, hidden_cols:]).astype(jnp.bfloat16)

time: 350 us -> 318 us (0.909)
  blocking collectives: 216 us -> 197 us
  waiting for transfers between devices: 60.1 us -> 51.3 us
  other arithmetic: 19.1 us -> 10.9 us
  matrix products: 11.8 us -> 16.2 us
    all_to_all x3 -> x1, blocking collectives: 85.5 us -> 47.9 us  [reduce_chips(): moved = lax.all_to_all(blocks.astype(link_type), 'dp', 0, 0, tiled=True)]
    all_gather x2, blocking collectives: 41.4 us -> 59.4 us  [chip_rows(): both = lax.all_gather(values, ('group', 'tensor'), axis=0, tiled=True)]
    reduce_sum x4 -> x2, other arithmetic: 12.9 us -> 0.58 us  [reduce_chips(): return jnp.sum(moved.astype(jnp.float32), axis=0)]
    all_gather x2, waiting for transfers between devices: 26.1 us -> 17.2 us  [gather_rows(): both = lax.all_gather(across, 'group', axis=0, tiled=True)]
    dot_general x4 -> x2, matrix products: 2.89 us -> 8.07 us  [the longest x1 5.16 us: per_device(): jnp.dot(gathered, ffn_weights, preferred_element_type=jnp.float32)]
    concatenate x2, other arithmetic: 1.51 us -> 6.35 us  [chip_weights(): jnp.concatenate(matrices, axis=1)]
  transfers between devices with their start and end apart: 5 -> 7, of which waited for: 5 -> 5; matrix products, arithmetic and copies ran while one was open for 0% -> 5% of each run, Pallas kernels for 0% -> 0%
where the time goes in v3:
time: 318 us; the launch traced here: 317 us
  blocking collectives  197 us (62%)
  waiting for transfers between devices  51.3 us (16%)
  starting transfers between devices  20 us (6%)
  matrix products  16.2 us (5%)
  between operations  13.4 us (4%)
  other arithmetic  10.9 us (3%)
  local copies, waits for them, and re-layouts  8.02 us (3%)
    all_gather x2, blocking collectives, chip_rows(): both = lax.all_gather(values, ('group', 'tensor'), axis=0, tiled=True)  59.4 us
    all_to_all x2, blocking collectives, reduce_rows(): return jnp.sum(lax.all_to_all(blocks, axis, 0, 0, tiled=True), axis=0)  48.1 us
    all_to_all x1, blocking collectives, reduce_chips(): moved = lax.all_to_all(blocks.astype(link_type), 'dp', 0, 0, tiled=True)  47.9 us
    all_to_all x2, blocking collectives, gather_rows(): lax.all_to_all(jnp.broadcast_to(values[None], (chips,) + values.shape), '...  41.8 us
    all_to_all x1, waiting for transfers between devices, reduce_chips(): moved = lax.all_to_all(blocks.astype(link_type), 'dp', 0, 0, tiled=True)  23.1 us
    all_gather x2, waiting for transfers between devices, gather_rows(): both = lax.all_gather(across, 'group', axis=0, tiled=True)  17.2 us
    all_to_all x2, starting transfers between devices, gather_width(): return lax.all_to_all(sent, WIDTH, 0, 0, tiled=True)  16.1 us
    all_to_all x2, waiting for transfers between devices, gather_width(): return lax.all_to_all(sent, WIDTH, 0, 0, tiled=True)  10.8 us
  transfers between devices with their start and end apart: 7, of which 5 were waited for; matrix products, arithmetic and copies ran while one was open for 5% of the time, Pallas kernels for 0%

profile of v3, /device:TPU:1, one launch (start us, length us, event | category | flops | bytes accessed | tf_op | source)
XLA Modules:
  0.0 317.1 jit_solution(2219621707964727382)
XLA Ops:
  6.5 0.8 convert_element_type.79
  7.3 0.9 fusion.6
  8.2 0.1 pad_maximum_fusion.2
  8.3 0.6 broadcast_in_dim.29
  8.9 8.6 %all-to-all-start = ((f32[32,1,80]{2,1,0:T(1,128)}), f32[32,1,80]{2,1,0:T(1,128)S(1)}, u32[]{:S(2)}, u32[]{:S(2)}) async-start(f32[32,1,80]{2,1,0:T(1,128)} %broadcast_in_dim.29), calls=%async_computation | async-start | bytes 32768 | tf_op jit(solution)/shard_map/all_to_all | solution.py:15
  17.5 0.0 all-gather.5.cloned.1.call-start
  17.6 2.0 pad_maximum_fusion.1
  19.6 0.0 all-gather.5.cloned.1.call-update
  19.6 0.7 convert_element_type.80
  20.3 4.0 %all-to-all-done = f32[32,1,80]{2,1,0:T(1,128)S(1)} async-done(((f32[32,1,80]{2,1,0:T(1,128)}), f32[32,1,80]{2,1,0:T(1,128)S(1)}, u32[]{:S(2)}, u32[]{:S(2)}) %all-to-all-start) | async-done | bytes 10272 | tf_op jit(solution)/shard_map/all_to_all | solution.py:15
  24.3 0.1 fusion.8
  24.4 32.2 %all_gather.18 = bf16[1024,256]{1,0:T(8,128)(2,1)S(1)} all-gather(bf16[64,256]{1,0:T(8,128)(2,1)S(1)} %fusion.8), channel_id=1, replica_groups=mesh['group'=2,'dp'=16,'tensor'=8] {'group','tensor'}, dimensions={0}, use_global_device_ids=true | all-gather | bytes 557056 | tf_op jit(solution)/shard_map/all_gather | solution.py:40
  56.6 0.5 copy.28
  57.2 0.1 copy.35
  57.2 0.1 slice_convert_fusion
  57.3 0.1 convert_element_type.83
  57.4 2.4 scatter_custom_fusion
  59.9 0.1 compare_select_fusion.1
  60.0 1.2 gather_fusion
  61.1 0.0 copy-start.3
  61.1 0.0 all-gather.5.cloned.1.call-done
  61.1 2.9 fusion.23
  64.0 3.7 %all-to-all-start.1 = ((f32[16,16,1280]{2,1,0:T(8,128)}), f32[16,16,1280]{2,1,0:T(8,128)S(1)}, u32[]{:S(2)}, u32[]{:S(2)}) async-start(f32[16,16,1280]{2,1,0:T(8,128)} %bitcast.59), calls=%async_computation.1 | async-start | bytes 2621440 | tf_op jit(solution)/shard_map/all_to_all | solution.py:35
  67.8 0.0 all-gather.7.cloned.1.call-start
  67.8 0.1 iota_compare_fusion
  67.9 23.1 %all-to-all-done.1 = f32[16,16,1280]{2,1,0:T(8,128)S(1)} async-done(((f32[16,16,1280]{2,1,0:T(8,128)}), f32[16,16,1280]{2,1,0:T(8,128)S(1)}, u32[]{:S(2)}, u32[]{:S(2)}) %all-to-all-start.1) | async-done | bytes 1310752 | tf_op jit(solution)/shard_map/all_to_all | solution.py:35
  91.0 0.1 reduce_sum.83
  91.1 0.1 fusion.14
  91.3 1.7 select_reduce_fusion
  93.0 0.2 fusion.5
  93.2 1.5 fusion.2
  94.7 0.1 broadcast_in_dim.33
  94.8 13.9 %all_to_all.45 = bf16[16,16,1024]{2,1,0:T(8,128)(2,1)} all-to-all(bf16[16,16,1024]{2,1,0:T(8,128)(2,1)S(1)} %broadcast_in_dim.33), channel_id=1, replica_groups=mesh['group'=2,'dp'=16,'tensor'=8] {'dp'}, dimensions={0} | all-to-all | bytes 1048576 | tf_op jit(solution)/shard_map/all_to_all | solution.py:25
  108.7 0.0 all-gather.7.cloned.1.call-update
  108.8 0.0 all-gather.9.cloned.1.call-start
  108.8 4.3 %pad_maximum_fusion = bf16[256,7168]{1,0:T(8,128)(2,1)} fusion(bf16[256,3584]{1,0:T(8,128)(2,1)} %param.19, bf16[256,3584]{1,0:T(8,128)(2,1)} %param.18), kind=kLoop, calls=%fused_computation.5 | loop fusion | flops 7340032 | bytes 7340032 | tf_op jit(solution)/shard_map/concatenate | solution.py:49
  113.1 0.0 all-gather.9.cloned.1.call-update
  113.2 4.4 %all-gather.7.cloned.1.call-done = bf16[32,16,1024]{2,1,0:T(8,128)(2,1)} async-done(((bf16[16,16,1024]{2,1,0:T(8,128)(2,1)}), bf16[32,16,1024]{2,1,0:T(8,128)(2,1)}) %all-gather.7.cloned.1.call-update) | async-done | bytes 1048592 | tf_op jit(solution)/shard_map/all_gather | solution.py:28
  117.6 0.0 copy-done.2
  117.6 1.7 fusion.24
  119.3 0.0 copy-start.4
  119.3 1.6 gather_fusion.1
  120.9 24.1 %all_to_all.46 = f32[8,64,256]{2,1,0:T(8,128)S(1)} all-to-all(f32[8,64,256]{2,1,0:T(8,128)S(1)} %bitcast.61), channel_id=1, replica_groups=mesh['group'=2,'dp'=16,'tensor'=8] {'tensor'}, dimensions={0} | all-to-all | bytes 1048576 | tf_op jit(solution)/shard_map/all_to_all | solution.py:55
  145.0 0.1 multiply_reduce_fusion
  145.1 0.6 broadcast_in_dim.34
  145.7 7.5 %all-to-all-start.4 = ((f32[32,1,64]{2,1,0:T(1,128)}), f32[32,1,64]{2,1,0:T(1,128)S(1)}, u32[]{:S(2)}, u32[]{:S(2)}) async-start(f32[32,1,64]{2,1,0:T(1,128)} %broadcast_in_dim.34), calls=%async_computation.4 | async-start | bytes 32768 | tf_op jit(solution)/shard_map/all_to_all | solution.py:15
  153.2 0.0 all-gather.11.cloned.1.call-start
  153.3 6.7 %all-to-all-done.4 = f32[32,1,64]{2,1,0:T(1,128)S(1)} async-done(((f32[32,1,64]{2,1,0:T(1,128)}), f32[32,1,64]{2,1,0:T(1,128)S(1)}, u32[]{:S(2)}, u32[]{:S(2)}) %all-to-all-start.4) | async-done | bytes 8224 | tf_op jit(solution)/shard_map/all_to_all | solution.py:15
  160.1 0.1 multiply_convert_fusion
  160.2 27.2 %all_gather.21 = bf16[1024,256]{1,0:T(8,128)(2,1)S(1)} all-gather(bf16[64,256]{1,0:T(8,128)(2,1)S(1)} %multiply_convert_fusion), channel_id=1, replica_groups=mesh['group'=2,'dp'=16,'tensor'=8] {'group','tensor'}, dimensions={0}, use_global_device_ids=true | all-gather | bytes 557056 | tf_op jit(solution)/shard_map/all_gather | solution.py:40
  187.4 0.5 copy.32
  187.9 0.1 copy.38
  188.0 0.0 all-gather.9.cloned.1.call-done
  188.0 5.2 %convolution_convert_fusion = bf16[256,7168]{1,0:T(8,128)(2,1)S(1)} fusion(bf16[512,7168]{1,0:T(8,128)(2,1)} %all-gather.9.cloned.1.call-done, bf16[512,512]{1,0:T(8,128)(2,1)S(1)} %bitcast.69, s32[]{:T(128)S(6)} %select_n.28), kind=kOutput, calls=%fused_computation.3 | convolution fusion | flops 1880883200 | bytes 11272196 | tf_op jit(solution)/shard_map/dot_general | solution.py:141
  193.2 47.9 %all_to_all.47 = bf16[16,16,7168]{2,1,0:T(8,128)(2,1)S(1)} all-to-all(bf16[16,16,7168]{2,1,0:T(8,128)(2,1)S(1)} %bitcast.60), channel_id=1, replica_groups=mesh['group'=2,'dp'=16,'tensor'=8] {'dp'}, dimensions={0} | all-to-all | bytes 7340032 | tf_op jit(solution)/shard_map/all_to_all | solution.py:35
  241.2 0.5 convert_reduce_fusion
  241.7 0.1 fusion.4
  241.8 0.2 broadcast_in_dim.35
  241.9 27.9 %all_to_all.48 = bf16[16,16,3584]{2,1,0:T(8,128)(2,1)} all-to-all(bf16[16,16,3584]{2,1,0:T(8,128)(2,1)S(1)} %broadcast_in_dim.35), channel_id=1, replica_groups=mesh['group'=2,'dp'=16,'tensor'=8] {'dp'}, dimensions={0} | all-to-all | bytes 3670016 | tf_op jit(solution)/shard_map/all_to_all | solution.py:25
  269.8 0.0 all-gather.11.cloned.1.call-update
  269.8 12.8 %all-gather.11.cloned.1.call-done = bf16[32,16,3584]{2,1,0:T(8,128)(2,1)} async-done(((bf16[16,16,3584]{2,1,0:T(8,128)(2,1)}), bf16[32,16,3584]{2,1,0:T(8,128)(2,1)}) %all-gather.11.cloned.1.call-update) | async-done | bytes 3670032 | tf_op jit(solution)/shard_map/all_gather | solution.py:28
  282.6 3.1 fusion
  285.8 24.1 %all_to_all.49 = f32[8,64,256]{2,1,0:T(8,128)S(1)} all-to-all(f32[8,64,256]{2,1,0:T(8,128)S(1)} %fusion), channel_id=1, replica_groups=mesh['group'=2,'dp'=16,'tensor'=8] {'tensor'}, dimensions={0} | all-to-all | bytes 1048576 | tf_op jit(solution)/shard_map/all_to_all | solution.py:55
  309.9 0.6 fusion.13
  (25 shorter events, 0.2 us)
Async XLA Ops:
  6.5 276.1 %copy-start = (bf16[3584,256]{1,0:T(8,128)(2,1)S(1)}, bf16[3584,256]{1,0:T(8,128)(2,1)}, u32[]{:S(2)}) copy-start(bf16[3584,256]{1,0:T(8,128)(2,1)} %param.20) | copy-start | bytes 5505028
  6.5 17.8 %copy-start.1 = (bf16[64,256]{1,0:T(8,128)(2,1)S(1)}, bf16[64,256]{1,0:T(8,128)(2,1)}, u32[]{:S(2)}) copy-start(bf16[64,256]{1,0:T(8,128)(2,1)} %param.12) | copy-start | bytes 98308
  8.9 15.4 %all-to-all-start = ((f32[32,1,80]{2,1,0:T(1,128)}), f32[32,1,80]{2,1,0:T(1,128)S(1)}, u32[]{:S(2)}, u32[]{:S(2)}) async-start(f32[32,1,80]{2,1,0:T(1,128)} %broadcast_in_dim.29), calls=%async_computation | async-start | bytes 32768 | tf_op jit(solution)/shard_map/all_to_all | solution.py:15
  17.5 43.6 %all-gather.5.cloned.1.call-start = ((), (), s32[]{:S(2)}) async-start(), calls=%async_computation.8 | async-start | bytes 1966080 | tf_op jit(solution)/shard_map/all_gather | solution.py:49
  61.1 6.7 %copy-start.3 = (s32[16]{0:T(128)S(1)}, s32[16]{0:T(128)}, u32[]{:S(2)}) copy-start(s32[16]{0:T(128)} %param.22) | copy-start | bytes 196
  64.0 27.0 %all-to-all-start.1 = ((f32[16,16,1280]{2,1,0:T(8,128)}), f32[16,16,1280]{2,1,0:T(8,128)S(1)}, u32[]{:S(2)}, u32[]{:S(2)}) async-start(f32[16,16,1280]{2,1,0:T(8,128)} %bitcast.59), calls=%async_computation.1 | async-start | bytes 2621440 | tf_op jit(solution)/shard_map/all_to_all | solution.py:35
  67.8 49.8 %all-gather.7.cloned.1.call-start = ((), (), s32[]{:S(2)}) async-start(), calls=%async_computation.9 | async-start | bytes 1572864 | tf_op jit(solution)/shard_map/all_gather | solution.py:28
  108.8 79.3 %all-gather.9.cloned.1.call-start = ((), (), s32[]{:S(2)}) async-start(), calls=%async_computation.10 | async-start | bytes 11010048 | tf_op jit(solution)/shard_map/all_gather | solution.py:49
  113.1 4.5 %copy-start.2 = (bf16[1024,256]{1,0:T(8,128)(2,1)S(1)}, bf16[1024,256]{1,0:T(8,128)(2,1)}, u32[]{:S(2)}) copy-start(bf16[1024,256]{1,0:T(8,128)(2,1)} %param.17) | copy-start | bytes 1572868
  119.3 34.0 %copy-start.4 = (bf16[256]{0:T(256)(128)(2,1)S(1)}, bf16[256]{0:T(256)(128)(2,1)}, u32[]{:S(2)}) copy-start(bf16[256]{0:T(256)(128)(2,1)} %param.14) | copy-start | bytes 1540
  145.7 14.3 %all-to-all-start.4 = ((f32[32,1,64]{2,1,0:T(1,128)}), f32[32,1,64]{2,1,0:T(1,128)S(1)}, u32[]{:S(2)}, u32[]{:S(2)}) async-start(f32[32,1,64]{2,1,0:T(1,128)} %broadcast_in_dim.34), calls=%async_computation.4 | async-start | bytes 32768 | tf_op jit(solution)/shard_map/all_to_all | solution.py:15
  153.2 129.4 %all-gather.11.cloned.1.call-start = ((), (), s32[]{:S(2)}) async-start(), calls=%async_computation.11 | async-start | bytes 5505024 | tf_op jit(solution)/shard_map/all_gather | solution.py:28
Sparse Core Ops, SparseCore 0:
  20.1 18.0 all-gather.4
  108.9 8.6 all-gather.6
  119.4 24.9 all-gather.8
  270.0 12.6 all-gather.10

commit v4 on v3

--- a/solution.py
+++ b/solution.py
@@ -36,13 +36,18 @@
     return jnp.sum(moved.astype(jnp.float32), axis=0)
 
 
-def chip_rows(values):
-    both = lax.all_gather(values, ("group", "tensor"), axis=0, tiled=True)
+def chip_blocks(values):
     cores = lax.axis_size("group")
     parts = lax.axis_size("tensor")
-    rows, width = values.shape
-    both = both.reshape(cores, parts, rows, width).transpose(1, 2, 0, 3)
-    return both.reshape(parts * rows, cores * width)
+    sent = jnp.broadcast_to(values[None], (cores * parts,) + values.shape)
+    got = lax.all_to_all(sent, ("group", "tensor"), 0, 0, tiled=True)
+    return got.reshape((cores, parts) + values.shape)
+
+
+def chip_rows(values):
+    blocks = chip_blocks(values)
+    cores, parts, rows, width = blocks.shape
+    return blocks.transpose(1, 2, 0, 3).reshape(parts * rows, cores * width)
 
 
 def chip_weights(matrices):
@@ -109,9 +114,15 @@
     resid = stream.astype(jnp.float32)
 
     own_squares = jnp.sum(resid * resid, axis=1)
-    shared = gather_width(jnp.concatenate([own_squares, location.astype(jnp.float32)]))
-    squares = jnp.sum(shared[:, :rows], axis=0)
-    where = shared[:, rows:].reshape(-1).astype(jnp.int32)
+    everyone = ("group", "dp", "tensor")
+    devices = lax.axis_size(everyone)
+    parts = lax.axis_size("tensor")
+    payload = jnp.concatenate([own_squares, location.astype(jnp.float32)])
+    shared = lax.all_to_all(
+        jnp.broadcast_to(payload[None], (devices, payload.shape[0])), everyone, 0, 0, tiled=True
+    ).reshape(devices // parts, parts, -1)
+    all_squares = jnp.sum(shared[:, :, :rows], axis=0).reshape(-1)
+    where = shared[:, 0, rows:].reshape(-1).astype(jnp.int32)
     requests = where.shape[0]
     by_slot = jnp.zeros((requests,), jnp.int32).at[where].set(jnp.arange(requests, dtype=jnp.int32))
 
@@ -120,9 +131,12 @@
     qkv_weights = chip_weights((w_query, w_keyval))
     ffn_weights = chip_weights((w_gate, w_up))
 
-    attn_in = scale_rows(resid, squares, norm_attn)
+    blocks = chip_blocks(jnp.concatenate([stream, norm_attn[None, :]], axis=0))
+    cores = blocks.shape[0]
+    raw = blocks[:, :, :rows].transpose(1, 2, 0, 3).reshape(parts * rows, cores * blocks.shape[3])
+    gain = blocks[:, 0, rows].reshape(-1)
     mine = lax.dynamic_slice_in_dim(by_slot, core * half, half)
-    gathered = chip_rows(attn_in)[mine]
+    gathered = scale_rows(raw[mine].astype(jnp.float32), all_squares[mine], gain)
     joined = jnp.dot(gathered, qkv_weights, preferred_element_type=jnp.float32)
     summed = reduce_chips(joined, jnp.float32)
     query_cols = w_query.shape[1]

time: 318 us -> 316 us (level)
  blocking collectives: 197 us -> 155 us
  waiting for transfers between devices: 51.3 us -> 77.3 us
  starting transfers between devices: 20 us -> 31.4 us
  local copies, waits for them, and re-layouts: 8.02 us -> 11.7 us
    all_gather x2 -> x0, blocking collectives: 59.4 us -> none  [chip_rows(): both = lax.all_gather(values, ('group', 'tensor'), axis=0, tiled=True)]
    all_to_all x0 -> x2, waiting for transfers between devices: none -> 21.5 us  [the longest x1 11.4 us: per_device(): lax.all_to_all(jnp.broadcast_to(payload[None], (devices, payload.shape[0]...]
    all_to_all x0 -> x2, starting transfers between devices: none -> 19.7 us  [the longest x1 15.6 us: per_device(): lax.all_to_all(jnp.broadcast_to(payload[None], (devices, payload.shape[0]...]
    all_to_all x0 -> x1, blocking collectives: none -> 18 us  [chip_blocks(): got = lax.all_to_all(sent, ('group', 'tensor'), 0, 0, tiled=True)]
    all_gather x2, waiting for transfers between devices: 17.2 us -> 29.3 us  [gather_rows(): both = lax.all_gather(across, 'group', axis=0, tiled=True)]
    all_to_all x2 -> x1, starting transfers between devices: 16.1 us -> 7.51 us  [gather_width(): return lax.all_to_all(sent, WIDTH, 0, 0, tiled=True)]
    all_to_all x2 -> x1, waiting for transfers between devices: 10.8 us -> 6.74 us  [gather_width(): return lax.all_to_all(sent, WIDTH, 0, 0, tiled=True)]
    all_to_all x1, waiting for transfers between devices: 23.1 us -> 19.6 us  [reduce_chips(): moved = lax.all_to_all(blocks.astype(link_type), 'dp', 0, 0, tiled=True)]
  transfers between devices with their start and end apart: 7 -> 8, of which waited for: 5 -> 6; matrix products, arithmetic and copies ran while one was open for 5% -> 6% of each run, Pallas kernels for 0% -> 0%
where the time goes in v4:
time: 316 us; the launch traced here: 315 us
  blocking collectives  155 us (49%)
  waiting for transfers between devices  77.3 us (24%)
  starting transfers between devices  31.4 us (10%)
  matrix products  16.3 us (5%)
  between operations  13.5 us (4%)
  local copies, waits for them, and re-layouts  11.7 us (4%)
  other arithmetic  9.88 us (3%)
    all_to_all x2, blocking collectives, reduce_rows(): return jnp.sum(lax.all_to_all(blocks, axis, 0, 0, tiled=True), axis=0)  48.1 us
    all_to_all x1, blocking collectives, reduce_chips(): moved = lax.all_to_all(blocks.astype(link_type), 'dp', 0, 0, tiled=True)  46.8 us
    all_to_all x2, blocking collectives, gather_rows(): lax.all_to_all(jnp.broadcast_to(values[None], (chips,) + values.shape), '...  42.2 us
    all_gather x2, waiting for transfers between devices, gather_rows(): both = lax.all_gather(across, 'group', axis=0, tiled=True)  29.3 us
    all_to_all x1, waiting for transfers between devices, reduce_chips(): moved = lax.all_to_all(blocks.astype(link_type), 'dp', 0, 0, tiled=True)  19.6 us
    all_to_all x1, blocking collectives, chip_blocks(): got = lax.all_to_all(sent, ('group', 'tensor'), 0, 0, tiled=True)  18 us
    all_to_all x1, starting transfers between devices, per_device(): lax.all_to_all(jnp.broadcast_to(payload[None], (devices, payload.shape[0]...  15.6 us
    all_to_all x1, waiting for transfers between devices, per_device(): lax.all_to_all(jnp.broadcast_to(payload[None], (devices, payload.shape[0]...  11.4 us
  transfers between devices with their start and end apart: 8, of which 6 were waited for; matrix products, arithmetic and copies ran while one was open for 6% of the time, Pallas kernels for 0%

profile of v4, /device:TPU:1, one launch (start us, length us, event | category | flops | bytes accessed | tf_op | source)
XLA Modules:
  0.0 315.1 jit_solution(3298619285379074111)
XLA Ops:
  6.5 0.8 convert_element_type.89
  7.3 0.9 fusion.9
  8.2 0.1 pad_maximum_fusion.3
  8.3 0.7 broadcast_in_dim.37
  9.0 15.6 %all-to-all-start.1 = ((f32[256,1,80]{2,1,0:T(1,128)}), f32[256,1,80]{2,1,0:T(1,128)S(1)}, u32[]{:S(2)}, u32[]{:S(2)}) async-start(f32[256,1,80]{2,1,0:T(1,128)} %broadcast_in_dim.37), calls=%async_computation.1 | async-start | bytes 262144 | tf_op jit(solution)/shard_map/all_to_all | solution.py:121
  24.7 0.7 broadcast_in_dim.35
  25.3 0.8 pad_maximum_fusion.2
  26.1 11.4 %all-to-all-done.1 = f32[256,1,80]{2,1,0:T(1,128)S(1)} async-done(((f32[256,1,80]{2,1,0:T(1,128)}), f32[256,1,80]{2,1,0:T(1,128)S(1)}, u32[]{:S(2)}, u32[]{:S(2)}) %all-to-all-start.1) | async-done | bytes 81952 | tf_op jit(solution)/shard_map/all_to_all | solution.py:121
  37.5 0.8 broadcast_in_dim.36
  38.4 4.1 %all-to-all-start = ((bf16[16,65,256]{2,1,0:T(8,128)(2,1)}), bf16[16,65,256]{2,1,0:T(8,128)(2,1)S(1)}, u32[]{:S(2)}, u32[]{:S(2)}) async-start(bf16[16,65,256]{2,1,0:T(8,128)(2,1)} %broadcast_in_dim.36), calls=%async_computation | async-start | bytes 1179648 | tf_op jit(solution)/shard_map/all_to_all | solution.py:43
  42.4 0.0 all-gather.5.cloned.1.call-start
  42.5 0.9 pad_maximum_fusion.1
  43.4 0.1 fusion.15
  43.6 0.1 convert_element_type.91
  43.7 0.1 reshape.191
  43.8 2.4 scatter_custom_fusion
  46.2 0.1 compare_select_fusion.1
  46.3 1.9 gather_fusion.1
  48.3 10.1 %all-to-all-done = bf16[16,65,256]{2,1,0:T(8,128)(2,1)S(1)} async-done(((bf16[16,65,256]{2,1,0:T(8,128)(2,1)}), bf16[16,65,256]{2,1,0:T(8,128)(2,1)S(1)}, u32[]{:S(2)}, u32[]{:S(2)}) %all-to-all-start) | async-done | bytes 532512 | tf_op jit(solution)/shard_map/all_to_all | solution.py:43
  58.4 0.1 copy.48
  58.5 0.4 copy.33
  58.9 0.1 copy.40
  59.0 1.2 gather_fusion
  60.2 0.0 all-gather.5.cloned.1.call-done
  60.2 3.0 fusion.3
  63.2 4.0 %all-to-all-start.2 = ((f32[16,16,1280]{2,1,0:T(8,128)}), f32[16,16,1280]{2,1,0:T(8,128)S(1)}, u32[]{:S(2)}, u32[]{:S(2)}) async-start(f32[16,16,1280]{2,1,0:T(8,128)} %bitcast.63), calls=%async_computation.2 | async-start | bytes 2621440 | tf_op jit(solution)/shard_map/all_to_all | solution.py:35
  67.2 0.0 all-gather.7.cloned.1.call-start
  67.2 0.1 iota_compare_fusion
  67.3 19.6 %all-to-all-done.2 = f32[16,16,1280]{2,1,0:T(8,128)S(1)} async-done(((f32[16,16,1280]{2,1,0:T(8,128)}), f32[16,16,1280]{2,1,0:T(8,128)S(1)}, u32[]{:S(2)}, u32[]{:S(2)}) %all-to-all-start.2) | async-done | bytes 1310752 | tf_op jit(solution)/shard_map/all_to_all | solution.py:35
  86.9 0.1 reduce_sum.83
  87.0 0.1 fusion.16
  87.1 1.7 select_reduce_fusion
  88.8 0.2 fusion.8
  89.0 1.5 fusion.2
  90.6 0.1 broadcast_in_dim.41
  90.7 15.2 %all_to_all.52 = bf16[16,16,1024]{2,1,0:T(8,128)(2,1)} all-to-all(bf16[16,16,1024]{2,1,0:T(8,128)(2,1)S(1)} %broadcast_in_dim.41), channel_id=1, replica_groups=mesh['group'=2,'dp'=16,'tensor'=8] {'dp'}, dimensions={0} | all-to-all | bytes 1048576 | tf_op jit(solution)/shard_map/all_to_all | solution.py:25
  105.8 0.0 all-gather.7.cloned.1.call-update
  105.9 0.0 all-gather.9.cloned.1.call-start
  105.9 4.3 %pad_maximum_fusion = bf16[256,7168]{1,0:T(8,128)(2,1)} fusion(bf16[256,3584]{1,0:T(8,128)(2,1)} %param.19, bf16[256,3584]{1,0:T(8,128)(2,1)} %param.18), kind=kLoop, calls=%fused_computation.6 | loop fusion | flops 7340032 | bytes 7340032 | tf_op jit(solution)/shard_map/concatenate | solution.py:54
  110.3 9.8 %all-gather.7.cloned.1.call-done = bf16[32,16,1024]{2,1,0:T(8,128)(2,1)} async-done(((bf16[16,16,1024]{2,1,0:T(8,128)(2,1)}), bf16[32,16,1024]{2,1,0:T(8,128)(2,1)}) %all-gather.7.cloned.1.call-update) | async-done | bytes 1048592 | tf_op jit(solution)/shard_map/all_gather | solution.py:28
  120.1 1.7 fusion.25
  121.8 1.6 gather_fusion.2
  123.4 24.1 %all_to_all.53 = f32[8,64,256]{2,1,0:T(8,128)S(1)} all-to-all(f32[8,64,256]{2,1,0:T(8,128)S(1)} %bitcast.67), channel_id=1, replica_groups=mesh['group'=2,'dp'=16,'tensor'=8] {'tensor'}, dimensions={0} | all-to-all | bytes 1048576 | tf_op jit(solution)/shard_map/all_to_all | solution.py:60
  147.5 0.1 multiply_reduce_fusion
  147.6 0.6 broadcast_in_dim.42
  148.3 7.5 %all-to-all-start.5 = ((f32[32,1,64]{2,1,0:T(1,128)}), f32[32,1,64]{2,1,0:T(1,128)S(1)}, u32[]{:S(2)}, u32[]{:S(2)}) async-start(f32[32,1,64]{2,1,0:T(1,128)} %broadcast_in_dim.42), calls=%async_computation.5 | async-start | bytes 32768 | tf_op jit(solution)/shard_map/all_to_all | solution.py:15
  155.8 0.0 all-gather.11.cloned.1.call-start
  155.8 6.7 %all-to-all-done.5 = f32[32,1,64]{2,1,0:T(1,128)S(1)} async-done(((f32[32,1,64]{2,1,0:T(1,128)}), f32[32,1,64]{2,1,0:T(1,128)S(1)}, u32[]{:S(2)}, u32[]{:S(2)}) %all-to-all-start.5) | async-done | bytes 8224 | tf_op jit(solution)/shard_map/all_to_all | solution.py:15
  162.6 0.1 multiply_convert_fusion.2
  162.8 18.0 %all_to_all.54 = bf16[16,64,256]{2,1,0:T(8,128)(2,1)S(1)} all-to-all(bf16[16,64,256]{2,1,0:T(8,128)(2,1)S(1)} %broadcast_in_dim.43), channel_id=1, replica_groups=mesh['group'=2,'dp'=16,'tensor'=8] {'group','tensor'}, dimensions={0} | all-to-all | bytes 1048576 | tf_op jit(solution)/shard_map/all_to_all | solution.py:43
  180.7 0.5 copy.37
  181.3 0.1 copy.43
  181.4 0.0 all-gather.9.cloned.1.call-done
  181.4 5.2 %convolution_convert_fusion = bf16[256,7168]{1,0:T(8,128)(2,1)S(1)} fusion(bf16[512,7168]{1,0:T(8,128)(2,1)} %all-gather.9.cloned.1.call-done, bf16[512,512]{1,0:T(8,128)(2,1)S(1)} %bitcast.76, s32[]{:T(128)S(6)} %select_n.29), kind=kOutput, calls=%fused_computation.4 | convolution fusion | flops 1880883200 | bytes 11272196 | tf_op jit(solution)/shard_map/dot_general | solution.py:155
  186.6 46.8 %all_to_all.55 = bf16[16,16,7168]{2,1,0:T(8,128)(2,1)S(1)} all-to-all(bf16[16,16,7168]{2,1,0:T(8,128)(2,1)S(1)} %bitcast.64), channel_id=1, replica_groups=mesh['group'=2,'dp'=16,'tensor'=8] {'dp'}, dimensions={0} | all-to-all | bytes 7340032 | tf_op jit(solution)/shard_map/all_to_all | solution.py:35
  233.4 0.5 convert_reduce_fusion
  233.9 0.1 fusion.7
  234.0 0.2 broadcast_in_dim.44
  234.1 27.0 %all_to_all.56 = bf16[16,16,3584]{2,1,0:T(8,128)(2,1)} all-to-all(bf16[16,16,3584]{2,1,0:T(8,128)(2,1)S(1)} %broadcast_in_dim.44), channel_id=1, replica_groups=mesh['group'=2,'dp'=16,'tensor'=8] {'dp'}, dimensions={0} | all-to-all | bytes 3670016 | tf_op jit(solution)/shard_map/all_to_all | solution.py:25
  261.1 0.0 all-gather.11.cloned.1.call-update
  261.2 19.5 %all-gather.11.cloned.1.call-done = bf16[32,16,3584]{2,1,0:T(8,128)(2,1)} async-done(((bf16[16,16,3584]{2,1,0:T(8,128)(2,1)}), bf16[32,16,3584]{2,1,0:T(8,128)(2,1)}) %all-gather.11.cloned.1.call-update) | async-done | bytes 3670032 | tf_op jit(solution)/shard_map/all_gather | solution.py:28
  280.7 3.1 fusion
  283.8 24.1 %all_to_all.57 = f32[8,64,256]{2,1,0:T(8,128)S(1)} all-to-all(f32[8,64,256]{2,1,0:T(8,128)S(1)} %fusion), channel_id=1, replica_groups=mesh['group'=2,'dp'=16,'tensor'=8] {'tensor'}, dimensions={0} | all-to-all | bytes 1048576 | tf_op jit(solution)/shard_map/all_to_all | solution.py:60
  307.9 0.6 fusion.14
  (37 shorter events, 0.4 us)
Async XLA Ops:
  6.5 274.1 %copy-start = (bf16[3584,256]{1,0:T(8,128)(2,1)S(1)}, bf16[3584,256]{1,0:T(8,128)(2,1)}, u32[]{:S(2)}) copy-start(bf16[3584,256]{1,0:T(8,128)(2,1)} %param.20) | copy-start | bytes 5505028
  6.5 36.0 %copy-start.4 = (bf16[256,256]{1,0:T(8,128)(2,1)S(1)}, bf16[256,256]{1,0:T(8,128)(2,1)}, u32[]{:S(2)}) copy-start(bf16[256,256]{1,0:T(8,128)(2,1)} %param.16) | copy-start | bytes 393220
  6.5 36.0 %copy-start.2 = (bf16[256,1024]{1,0:T(8,128)(2,1)S(1)}, bf16[256,1024]{1,0:T(8,128)(2,1)}, u32[]{:S(2)}) copy-start(bf16[256,1024]{1,0:T(8,128)(2,1)} %param.15) | copy-start | bytes 1572868
  9.0 28.5 %all-to-all-start.1 = ((f32[256,1,80]{2,1,0:T(1,128)}), f32[256,1,80]{2,1,0:T(1,128)S(1)}, u32[]{:S(2)}, u32[]{:S(2)}) async-start(f32[256,1,80]{2,1,0:T(1,128)} %broadcast_in_dim.37), calls=%async_computation.1 | async-start | bytes 262144 | tf_op jit(solution)/shard_map/all_to_all | solution.py:121
  38.4 20.0 %all-to-all-start = ((bf16[16,65,256]{2,1,0:T(8,128)(2,1)}), bf16[16,65,256]{2,1,0:T(8,128)(2,1)S(1)}, u32[]{:S(2)}, u32[]{:S(2)}) async-start(bf16[16,65,256]{2,1,0:T(8,128)(2,1)} %broadcast_in_dim.36), calls=%async_computation | async-start | bytes 1179648 | tf_op jit(solution)/shard_map/all_to_all | solution.py:43
  42.4 17.8 %all-gather.5.cloned.1.call-start = ((), (), s32[]{:S(2)}) async-start(), calls=%async_computation.10 | async-start | bytes 1966080 | tf_op jit(solution)/shard_map/all_gather | solution.py:54
  60.2 7.0 %copy-start.5 = (s32[16]{0:T(128)S(1)}, s32[16]{0:T(128)}, u32[]{:S(2)}) copy-start(s32[16]{0:T(128)} %param.22) | copy-start | bytes 196
  63.2 23.7 %all-to-all-start.2 = ((f32[16,16,1280]{2,1,0:T(8,128)}), f32[16,16,1280]{2,1,0:T(8,128)S(1)}, u32[]{:S(2)}, u32[]{:S(2)}) async-start(f32[16,16,1280]{2,1,0:T(8,128)} %bitcast.63), calls=%async_computation.2 | async-start | bytes 2621440 | tf_op jit(solution)/shard_map/all_to_all | solution.py:35
  67.2 53.0 %all-gather.7.cloned.1.call-start = ((), (), s32[]{:S(2)}) async-start(), calls=%async_computation.11 | async-start | bytes 1572864 | tf_op jit(solution)/shard_map/all_gather | solution.py:28
  105.9 75.5 %all-gather.9.cloned.1.call-start = ((), (), s32[]{:S(2)}) async-start(), calls=%async_computation.12 | async-start | bytes 11010048 | tf_op jit(solution)/shard_map/all_gather | solution.py:54
  110.2 9.9 %copy-start.3 = (bf16[1024,256]{1,0:T(8,128)(2,1)S(1)}, bf16[1024,256]{1,0:T(8,128)(2,1)}, u32[]{:S(2)}) copy-start(bf16[1024,256]{1,0:T(8,128)(2,1)} %param.17) | copy-start | bytes 1572868
  121.8 25.7 %copy-start.1 = (bf16[64,256]{1,0:T(8,128)(2,1)S(1)}, bf16[64,256]{1,0:T(8,128)(2,1)}, u32[]{:S(2)}) copy-start(bf16[64,256]{1,0:T(8,128)(2,1)} %param.12) | copy-start | bytes 98308
  121.8 34.0 %copy-start.6 = (bf16[256]{0:T(256)(128)(2,1)S(1)}, bf16[256]{0:T(256)(128)(2,1)}, u32[]{:S(2)}) copy-start(bf16[256]{0:T(256)(128)(2,1)} %param.14) | copy-start | bytes 1540
  148.3 14.3 %all-to-all-start.5 = ((f32[32,1,64]{2,1,0:T(1,128)}), f32[32,1,64]{2,1,0:T(1,128)S(1)}, u32[]{:S(2)}, u32[]{:S(2)}) async-start(f32[32,1,64]{2,1,0:T(1,128)} %broadcast_in_dim.42), calls=%async_computation.5 | async-start | bytes 32768 | tf_op jit(solution)/shard_map/all_to_all | solution.py:15
  155.8 124.9 %all-gather.11.cloned.1.call-start = ((), (), s32[]{:S(2)}) async-start(), calls=%async_computation.13 | async-start | bytes 5505024 | tf_op jit(solution)/shard_map/all_gather | solution.py:28
Sparse Core Ops, SparseCore 0:
  45.0 12.8 all-gather.4
  106.0 14.0 all-gather.6
  121.9 24.9 all-gather.8
  261.3 19.3 all-gather.10

commit v5 on v4

--- a/solution.py
+++ b/solution.py
@@ -25,7 +25,10 @@
     across = lax.all_to_all(
         jnp.broadcast_to(values[None], (chips,) + values.shape), "dp", 0, 0, tiled=True
     )
-    both = lax.all_gather(across, "group", axis=0, tiled=True)
+    cores = lax.axis_size("group")
+    both = lax.all_to_all(
+        jnp.broadcast_to(across[None], (cores,) + across.shape), "group", 0, 0, tiled=True
+    )
     return both.reshape((-1,) + values.shape[1:])
 
 
@@ -113,17 +116,28 @@
     rows = stream.shape[0]
     resid = stream.astype(jnp.float32)
 
-    own_squares = jnp.sum(resid * resid, axis=1)
-    everyone = ("group", "dp", "tensor")
-    devices = lax.axis_size(everyone)
+    width = stream.shape[1]
     parts = lax.axis_size("tensor")
-    payload = jnp.concatenate([own_squares, location.astype(jnp.float32)])
+    per_owner = location.shape[0]
+    pieces = jnp.concatenate([location // per_owner, location % per_owner]).astype(jnp.bfloat16)
+    extra = jnp.zeros((width,), jnp.bfloat16).at[: 2 * per_owner].set(pieces)
+    blocks = chip_blocks(jnp.concatenate([stream, norm_attn[None, :], extra[None, :]], axis=0))
+    cores = blocks.shape[0]
+    raw = blocks[:, :, :rows].transpose(1, 2, 0, 3).reshape(parts * rows, cores * width)
+    raw = raw.astype(jnp.float32)
+    gain = blocks[:, 0, rows].reshape(-1)
+    halves = blocks[:, 0, rows + 1, : 2 * per_owner].astype(jnp.float32).reshape(cores, 2, per_owner)
+    chip_where = halves[:, 0] * per_owner + halves[:, 1]
+    chip_squares = jnp.sum(raw * raw, axis=1)
+    chips = lax.axis_size("dp")
+    payload = jnp.concatenate([chip_squares, chip_where.reshape(-1)])
     shared = lax.all_to_all(
-        jnp.broadcast_to(payload[None], (devices, payload.shape[0])), everyone, 0, 0, tiled=True
-    ).reshape(devices // parts, parts, -1)
-    all_squares = jnp.sum(shared[:, :, :rows], axis=0).reshape(-1)
-    where = shared[:, 0, rows:].reshape(-1).astype(jnp.int32)
-    requests = where.shape[0]
+        jnp.broadcast_to(payload[None], (chips, payload.shape[0])), "dp", 0, 0, tiled=True
+    )
+    requests = chip_squares.shape[0]
+    all_squares = jnp.sum(shared[:, :requests], axis=0)
+    where = shared[:, requests:].reshape(chips, cores, per_owner).transpose(1, 0, 2)
+    where = where.reshape(-1).astype(jnp.int32)
     by_slot = jnp.zeros((requests,), jnp.int32).at[where].set(jnp.arange(requests, dtype=jnp.int32))
 
     core = lax.axis_index("group")
@@ -131,12 +145,8 @@
     qkv_weights = chip_weights((w_query, w_keyval))
     ffn_weights = chip_weights((w_gate, w_up))
 
-    blocks = chip_blocks(jnp.concatenate([stream, norm_attn[None, :]], axis=0))
-    cores = blocks.shape[0]
-    raw = blocks[:, :, :rows].transpose(1, 2, 0, 3).reshape(parts * rows, cores * blocks.shape[3])
-    gain = blocks[:, 0, rows].reshape(-1)
     mine = lax.dynamic_slice_in_dim(by_slot, core * half, half)
-    gathered = scale_rows(raw[mine].astype(jnp.float32), all_squares[mine], gain)
+    gathered = scale_rows(raw[mine], all_squares[mine], gain)
     joined = jnp.dot(gathered, qkv_weights, preferred_element_type=jnp.float32)
     summed = reduce_chips(joined, jnp.float32)
     query_cols = w_query.shape[1]

time: 316 us -> 288 us (0.911)
  waiting for transfers between devices: 77.3 us -> 51 us
  matrix products: 16.3 us -> 13.1 us
    all_gather x2 -> x0, waiting for transfers between devices: 29.3 us -> none  [gather_rows(): both = lax.all_gather(across, 'group', axis=0, tiled=True)]
    all_to_all x0 -> x2, blocking collectives: none -> 16.7 us  [gather_rows(): lax.all_to_all(jnp.broadcast_to(across[None], (cores,) + across.shape), '...]
    all_to_all x2 -> x1, blocking collectives: 42.2 us -> 26.6 us  [gather_rows(): lax.all_to_all(jnp.broadcast_to(values[None], (chips,) + values.shape), '...]
    all_to_all x1, starting transfers between devices: 4.07 us -> 9.97 us  [chip_blocks(): got = lax.all_to_all(sent, ('group', 'tensor'), 0, 0, tiled=True)]
    all_to_all x1 -> x2, waiting for transfers between devices: 11.4 us -> 15.3 us  [the longest x1 9.49 us: gather_rows(): lax.all_to_all(jnp.broadcast_to(values[None], (chips,) + values.shape), '...]
    all_to_all x1 -> x2, starting transfers between devices: 15.6 us -> 12.2 us  [the longest x1 6.75 us: per_device(): lax.all_to_all(jnp.broadcast_to(payload[None], (chips, payload.shape[0]))...]
  transfers between devices with their start and end apart: 8 -> 7, of which waited for: 6 -> 5; matrix products, arithmetic and copies ran while one was open for 6% -> 9% of each run, Pallas kernels for 0% -> 0%
where the time goes in v5:
time: 288 us; the launch traced here: 287 us
  blocking collectives  155 us (54%)
  waiting for transfers between devices  51 us (18%)
  starting transfers between devices  31.3 us (11%)
  between operations  13.8 us (5%)
  local copies, waits for them, and re-layouts  13.3 us (5%)
  matrix products  13.1 us (5%)
  other arithmetic  10.4 us (4%)
    all_to_all x1, blocking collectives, reduce_chips(): moved = lax.all_to_all(blocks.astype(link_type), 'dp', 0, 0, tiled=True)  46.8 us
    all_to_all x2, blocking collectives, reduce_rows(): return jnp.sum(lax.all_to_all(blocks, axis, 0, 0, tiled=True), axis=0)  46.5 us
    all_to_all x1, blocking collectives, gather_rows(): lax.all_to_all(jnp.broadcast_to(values[None], (chips,) + values.shape), '...  26.6 us
    all_to_all x1, blocking collectives, chip_blocks(): got = lax.all_to_all(sent, ('group', 'tensor'), 0, 0, tiled=True)  18 us
    all_to_all x1, waiting for transfers between devices, reduce_chips(): moved = lax.all_to_all(blocks.astype(link_type), 'dp', 0, 0, tiled=True)  17.3 us
    all_to_all x2, blocking collectives, gather_rows(): lax.all_to_all(jnp.broadcast_to(across[None], (cores,) + across.shape), '...  16.7 us
    all_to_all x1, waiting for transfers between devices, chip_blocks(): got = lax.all_to_all(sent, ('group', 'tensor'), 0, 0, tiled=True)  11.5 us
    all_to_all x1, starting transfers between devices, chip_blocks(): got = lax.all_to_all(sent, ('group', 'tensor'), 0, 0, tiled=True)  9.97 us
  transfers between devices with their start and end apart: 7, of which 5 were waited for; matrix products, arithmetic and copies ran while one was open for 9% of the time, Pallas kernels for 0%

profile of v5, /device:TPU:1, one launch (start us, length us, event | category | flops | bytes accessed | tf_op | source)
XLA Modules:
  0.0 287.4 jit_solution(8751193857991613794)
XLA Ops:
  6.5 2.1 pad_maximum_fusion.1
  8.7 0.7 convert_bitcast_fusion.1
  9.4 0.7 broadcast_in_dim.39
  10.0 0.1 fusion.20
  10.1 0.8 pad_maximum_fusion.2
  10.9 0.9 broadcast_in_dim.40
  11.8 10.0 %all-to-all-start = ((bf16[16,66,256]{2,1,0:T(8,128)(2,1)}), bf16[16,66,256]{2,1,0:T(8,128)(2,1)S(1)}, u32[]{:S(2)}, u32[]{:S(2)}) async-start(bf16[16,66,256]{2,1,0:T(8,128)(2,1)} %broadcast_in_dim.40), calls=%async_computation | async-start | bytes 1179648 | tf_op jit(solution)/shard_map/all_to_all | solution.py:46
  21.8 0.0 all-gather.5.cloned.1.call-start
  21.8 4.3 %pad_maximum_fusion = bf16[256,7168]{1,0:T(8,128)(2,1)} fusion(bf16[256,3584]{1,0:T(8,128)(2,1)} %param.21, bf16[256,3584]{1,0:T(8,128)(2,1)} %param.20), kind=kLoop, calls=%fused_computation.6 | loop fusion | flops 7340032 | bytes 7340032 | tf_op jit(solution)/shard_map/concatenate | solution.py:57
  26.2 11.5 %all-to-all-done = bf16[16,66,256]{2,1,0:T(8,128)(2,1)S(1)} async-done(((bf16[16,66,256]{2,1,0:T(8,128)(2,1)}), bf16[16,66,256]{2,1,0:T(8,128)(2,1)S(1)}, u32[]{:S(2)}, u32[]{:S(2)}) %all-to-all-start) | async-done | bytes 540704 | tf_op jit(solution)/shard_map/all_to_all | solution.py:46
  37.7 0.1 copy.63
  37.8 0.1 convert_bitcast_fusion
  37.9 0.2 fusion.3
  38.1 0.1 reshape.256
  38.2 0.1 add.77
  38.3 0.1 copy.45
  38.4 0.1 reduce_sum.84
  38.5 0.7 broadcast_in_dim.41
  39.1 6.8 %all-to-all-start.1 = ((f32[16,1,544]{2,1,0:T(1,128)}), f32[16,1,544]{2,1,0:T(1,128)S(1)}, u32[]{:S(2)}, u32[]{:S(2)}) async-start(f32[16,1,544]{2,1,0:T(1,128)} %broadcast_in_dim.41), calls=%async_computation.1 | async-start | bytes 81920 | tf_op jit(solution)/shard_map/all_to_all | solution.py:134
  45.9 0.5 copy.44
  46.4 0.1 copy.54
  46.5 5.8 %all-to-all-done.1 = f32[16,1,544]{2,1,0:T(1,128)S(1)} async-done(((f32[16,1,544]{2,1,0:T(1,128)}), f32[16,1,544]{2,1,0:T(1,128)S(1)}, u32[]{:S(2)}, u32[]{:S(2)}) %all-to-all-start.1) | async-done | bytes 34848 | tf_op jit(solution)/shard_map/all_to_all | solution.py:134
  52.3 0.1 convert_element_type.122
  52.4 0.1 convert_element_type.124
  52.5 2.4 scatter_custom_fusion
  55.0 0.1 compare_select_fusion.1
  55.1 1.0 gather_fusion
  56.1 1.9 gather_fusion.1
  58.1 3.0 %fusion.4 = f32[256,1280]{1,0:T(8,128)} fusion(bf16[512,1280]{1,0:T(8,128)(2,1)} %all-gather.3.cloned.1.call-done, f32[256,512]{1,0:T(8,128)S(1)} %gather_fusion, f32[512]{0:T(512)S(1)} %bitcast.94, f32[256]{0:T(256)S(1)} %add_rsqrt_fusion), kind=kOutput, calls=%fused_computation.20 | convolution fusion | flops 335937536 | bytes 3148800 | tf_op jit(solution)/shard_map/dot_general | solution.py:150
  61.1 3.8 %all-to-all-start.2 = ((f32[16,16,1280]{2,1,0:T(8,128)}), f32[16,16,1280]{2,1,0:T(8,128)S(1)}, u32[]{:S(2)}, u32[]{:S(2)}) async-start(f32[16,16,1280]{2,1,0:T(8,128)} %bitcast.7), calls=%async_computation.2 | async-start | bytes 2621440 | tf_op jit(solution)/shard_map/all_to_all | solution.py:38
  64.9 0.1 iota_compare_fusion
  65.0 17.3 %all-to-all-done.2 = f32[16,16,1280]{2,1,0:T(8,128)S(1)} async-done(((f32[16,16,1280]{2,1,0:T(8,128)}), f32[16,16,1280]{2,1,0:T(8,128)S(1)}, u32[]{:S(2)}, u32[]{:S(2)}) %all-to-all-start.2) | async-done | bytes 1310752 | tf_op jit(solution)/shard_map/all_to_all | solution.py:38
  82.3 0.1 reduce_sum.86
  82.4 0.1 fusion.15
  82.6 1.7 select_reduce_fusion
  84.3 0.2 fusion.9
  84.5 1.5 fusion.2
  86.0 0.9 broadcast_in_dim.45
  86.9 5.4 %all-to-all-start.3 = ((bf16[16,16,1024]{2,1,0:T(8,128)(2,1)}), bf16[16,16,1024]{2,1,0:T(8,128)(2,1)S(1)}, u32[]{:S(2)}, u32[]{:S(2)}) async-start(bf16[16,16,1024]{2,1,0:T(8,128)(2,1)} %broadcast_in_dim.45), calls=%async_computation.3 | async-start | bytes 1048576 | tf_op jit(solution)/shard_map/all_to_all | solution.py:25
  92.4 9.5 %all-to-all-done.3 = bf16[16,16,1024]{2,1,0:T(8,128)(2,1)S(1)} async-done(((bf16[16,16,1024]{2,1,0:T(8,128)(2,1)}), bf16[16,16,1024]{2,1,0:T(8,128)(2,1)S(1)}, u32[]{:S(2)}, u32[]{:S(2)}) %all-to-all-start.3) | async-done | bytes 524320 | tf_op jit(solution)/shard_map/all_to_all | solution.py:25
  101.9 0.1 broadcast_in_dim.46
  102.0 7.2 %all_to_all.65 = bf16[2,16,16,1024]{3,2,1,0:T(8,128)(2,1)S(1)} all-to-all(bf16[2,16,16,1024]{3,2,1,0:T(8,128)(2,1)S(1)} %broadcast_in_dim.46), channel_id=1, replica_groups=mesh['group'=2,'dp'=16,'tensor'=8] {'group'}, dimensions={0} | all-to-all | bytes 2097152 | tf_op jit(solution)/shard_map/all_to_all | solution.py:29
  109.2 0.4 fusion.29
  109.7 1.6 gather_fusion.2
  111.3 22.7 %all_to_all.66 = f32[8,64,256]{2,1,0:T(8,128)S(1)} all-to-all(f32[8,64,256]{2,1,0:T(8,128)S(1)} %bitcast.78), channel_id=1, replica_groups=mesh['group'=2,'dp'=16,'tensor'=8] {'tensor'}, dimensions={0} | all-to-all | bytes 1048576 | tf_op jit(solution)/shard_map/all_to_all | solution.py:63
  134.0 0.1 multiply_reduce_fusion
  134.1 0.6 broadcast_in_dim.47
  134.7 5.3 %all-to-all-start.6 = ((f32[32,1,64]{2,1,0:T(1,128)}), f32[32,1,64]{2,1,0:T(1,128)S(1)}, u32[]{:S(2)}, u32[]{:S(2)}) async-start(f32[32,1,64]{2,1,0:T(1,128)} %broadcast_in_dim.47), calls=%async_computation.6 | async-start | bytes 32768 | tf_op jit(solution)/shard_map/all_to_all | solution.py:15
  140.1 6.7 %all-to-all-done.6 = f32[32,1,64]{2,1,0:T(1,128)S(1)} async-done(((f32[32,1,64]{2,1,0:T(1,128)}), f32[32,1,64]{2,1,0:T(1,128)S(1)}, u32[]{:S(2)}, u32[]{:S(2)}) %all-to-all-start.6) | async-done | bytes 8224 | tf_op jit(solution)/shard_map/all_to_all | solution.py:15
  146.8 0.1 multiply_convert_fusion.2
  147.0 18.0 %all_to_all.67 = bf16[16,64,256]{2,1,0:T(8,128)(2,1)S(1)} all-to-all(bf16[16,64,256]{2,1,0:T(8,128)(2,1)S(1)} %broadcast_in_dim.48), channel_id=1, replica_groups=mesh['group'=2,'dp'=16,'tensor'=8] {'group','tensor'}, dimensions={0} | all-to-all | bytes 1048576 | tf_op jit(solution)/shard_map/all_to_all | solution.py:46
  165.0 0.5 copy.50
  165.5 0.1 copy.57
  165.6 5.2 %convolution_convert_fusion = bf16[256,7168]{1,0:T(8,128)(2,1)S(1)} fusion(bf16[512,7168]{1,0:T(8,128)(2,1)} %all-gather.5.cloned.1.call-done, bf16[512,512]{1,0:T(8,128)(2,1)S(1)} %bitcast.83, s32[]{:T(128)S(6)} %select_n.43), kind=kOutput, calls=%fused_computation.4 | convolution fusion | flops 1880883200 | bytes 11272196 | tf_op jit(solution)/shard_map/dot_general | solution.py:165
  170.8 46.8 %all_to_all.68 = bf16[16,16,7168]{2,1,0:T(8,128)(2,1)S(1)} all-to-all(bf16[16,16,7168]{2,1,0:T(8,128)(2,1)S(1)} %bitcast.76), channel_id=1, replica_groups=mesh['group'=2,'dp'=16,'tensor'=8] {'dp'}, dimensions={0} | all-to-all | bytes 7340032 | tf_op jit(solution)/shard_map/all_to_all | solution.py:38
  217.6 0.5 convert_reduce_fusion
  218.1 0.1 fusion.8
  218.2 0.2 broadcast_in_dim.49
  218.4 26.6 %all_to_all.69 = bf16[16,16,3584]{2,1,0:T(8,128)(2,1)S(1)} all-to-all(bf16[16,16,3584]{2,1,0:T(8,128)(2,1)S(1)} %broadcast_in_dim.49), channel_id=1, replica_groups=mesh['group'=2,'dp'=16,'tensor'=8] {'dp'}, dimensions={0} | all-to-all | bytes 3670016 | tf_op jit(solution)/shard_map/all_to_all | solution.py:25
  245.0 0.4 broadcast_in_dim.50
  245.4 9.5 %all_to_all.70 = bf16[2,16,16,3584]{3,2,1,0:T(8,128)(2,1)S(1)} all-to-all(bf16[2,16,16,3584]{3,2,1,0:T(8,128)(2,1)S(1)} %broadcast_in_dim.50), channel_id=1, replica_groups=mesh['group'=2,'dp'=16,'tensor'=8] {'group'}, dimensions={0} | all-to-all | bytes 7340032 | tf_op jit(solution)/shard_map/all_to_all | solution.py:29
  254.9 1.1 fusion
  256.0 23.8 %all_to_all.71 = f32[8,64,256]{2,1,0:T(8,128)S(1)} all-to-all(f32[8,64,256]{2,1,0:T(8,128)S(1)} %fusion), channel_id=1, replica_groups=mesh['group'=2,'dp'=16,'tensor'=8] {'tensor'}, dimensions={0} | all-to-all | bytes 1048576 | tf_op jit(solution)/shard_map/all_to_all | solution.py:63
  279.9 0.6 fusion.14
  (41 shorter events, 0.4 us)
Async XLA Ops:
  6.5 248.4 %copy-start = (bf16[3584,256]{1,0:T(8,128)(2,1)S(1)}, bf16[3584,256]{1,0:T(8,128)(2,1)}, u32[]{:S(2)}) copy-start(bf16[3584,256]{1,0:T(8,128)(2,1)} %param.22) | copy-start | bytes 5505028
  6.5 51.5 %all-gather.3.cloned.1.call-start = ((), (), s32[]{:S(2)}) async-start(), calls=%async_computation.12 | async-start | bytes 1966080 | tf_op jit(solution)/shard_map/all_gather | solution.py:57
  11.8 25.9 %all-to-all-start = ((bf16[16,66,256]{2,1,0:T(8,128)(2,1)}), bf16[16,66,256]{2,1,0:T(8,128)(2,1)S(1)}, u32[]{:S(2)}, u32[]{:S(2)}) async-start(bf16[16,66,256]{2,1,0:T(8,128)(2,1)} %broadcast_in_dim.40), calls=%async_computation | async-start | bytes 1179648 | tf_op jit(solution)/shard_map/all_to_all | solution.py:46
  21.8 143.9 %all-gather.5.cloned.1.call-start = ((), (), s32[]{:S(2)}) async-start(), calls=%async_computation.13 | async-start | bytes 11010048 | tf_op jit(solution)/shard_map/all_gather | solution.py:57
  39.1 13.2 %all-to-all-start.1 = ((f32[16,1,544]{2,1,0:T(1,128)}), f32[16,1,544]{2,1,0:T(1,128)S(1)}, u32[]{:S(2)}, u32[]{:S(2)}) async-start(f32[16,1,544]{2,1,0:T(1,128)} %broadcast_in_dim.41), calls=%async_computation.1 | async-start | bytes 81920 | tf_op jit(solution)/shard_map/all_to_all | solution.py:134
  61.1 3.8 %copy-start.3 = (s32[16]{0:T(128)S(1)}, s32[16]{0:T(128)}, u32[]{:S(2)}) copy-start(s32[16]{0:T(128)} %param.24) | copy-start | bytes 196
  61.1 21.2 %all-to-all-start.2 = ((f32[16,16,1280]{2,1,0:T(8,128)}), f32[16,16,1280]{2,1,0:T(8,128)S(1)}, u32[]{:S(2)}, u32[]{:S(2)}) async-start(f32[16,16,1280]{2,1,0:T(8,128)} %bitcast.7), calls=%async_computation.2 | async-start | bytes 2621440 | tf_op jit(solution)/shard_map/all_to_all | solution.py:38
  86.9 15.0 %all-to-all-start.3 = ((bf16[16,16,1024]{2,1,0:T(8,128)(2,1)}), bf16[16,16,1024]{2,1,0:T(8,128)(2,1)S(1)}, u32[]{:S(2)}, u32[]{:S(2)}) async-start(bf16[16,16,1024]{2,1,0:T(8,128)(2,1)} %broadcast_in_dim.45), calls=%async_computation.3 | async-start | bytes 1048576 | tf_op jit(solution)/shard_map/all_to_all | solution.py:25
  92.3 16.9 %copy-start.2 = (bf16[1024,256]{1,0:T(8,128)(2,1)S(1)}, bf16[1024,256]{1,0:T(8,128)(2,1)}, u32[]{:S(2)}) copy-start(bf16[1024,256]{1,0:T(8,128)(2,1)} %param.19) | copy-start | bytes 1572868
  109.7 24.3 %copy-start.1 = (bf16[64,256]{1,0:T(8,128)(2,1)S(1)}, bf16[64,256]{1,0:T(8,128)(2,1)}, u32[]{:S(2)}) copy-start(bf16[64,256]{1,0:T(8,128)(2,1)} %param.14) | copy-start | bytes 98308
  109.7 30.4 %copy-start.4 = (bf16[256]{0:T(256)(128)(2,1)S(1)}, bf16[256]{0:T(256)(128)(2,1)}, u32[]{:S(2)}) copy-start(bf16[256]{0:T(256)(128)(2,1)} %param.16) | copy-start | bytes 1540
  134.7 12.1 %all-to-all-start.6 = ((f32[32,1,64]{2,1,0:T(1,128)}), f32[32,1,64]{2,1,0:T(1,128)S(1)}, u32[]{:S(2)}, u32[]{:S(2)}) async-start(f32[32,1,64]{2,1,0:T(1,128)} %broadcast_in_dim.47), calls=%async_computation.6 | async-start | bytes 32768 | tf_op jit(solution)/shard_map/all_to_all | solution.py:15
Sparse Core Ops, SparseCore 0:
  9.1 19.2 all-gather.2
  30.2 24.9 all-gather.4
